TPU v7x, 128 devices: a whole 4x4x4 slice. The times are simulated.
128 devices in a mesh: req: 4 (over z), seq: 32 (over x, y, core).
Axes of the slice: x: 4, y: 4, z: 4, core: 2. Of those that a mesh axis runs over, the one named last changes fastest.
Arguments:
- short_tokens: bfloat16 [256, 4, 1024], P(('req', 'seq')), may hold values from -6 to 6
- long_tokens: bfloat16 [8, 4, 1024], P('req'), may hold values from -6 to 6
- short_keys: bfloat16 [256, 1024, 1024], P(('req', 'seq'))
- short_values: bfloat16 [256, 1024, 1024], P(('req', 'seq')), may hold values from -6 to 6
- long_keys: bfloat16 [8, 8192, 1024], P('req', 'seq')
- long_values: bfloat16 [8, 8192, 1024], P('req', 'seq'), may hold values from -6 to 6
- short_lengths: int32 [256], P(('req', 'seq')), may hold values from 512 to 1024
- long_lengths: int32 [8], P('req'), may hold values from 4096 to 8192
- attn_gain: float32 [1024], replicated, may hold values from 0.5 to 1.5
- ffn_gain: float32 [1024], replicated, may hold values from 0.5 to 1.5
- w_query: bfloat16 [1024, 1024], P(None, 'req'), may hold values from -0.1875 to 0.1875
- w_key: bfloat16 [1024, 1024], P(None, 'req'), may hold values from -0.1875 to 0.1875
- w_value: bfloat16 [1024, 1024], P(None, 'req'), may hold values from -0.1875 to 0.1875
- w_out: bfloat16 [1024, 1024], P('req'), may hold values from -0.1875 to 0.1875
- w_up: bfloat16 [1024, 4096], P(None, 'req'), may hold values from -0.1875 to 0.1875
- w_down: bfloat16 [4096, 1024], P('req'), may hold values from -0.09375 to 0.09375
Outputs:
- short_hidden: bfloat16 [256, 4, 1024], P(('req', 'seq'))
- long_hidden: bfloat16 [8, 4, 1024], P('req')
- short_new_keys: bfloat16 [256, 4, 1024], P(('req', 'seq'))
- short_new_values: bfloat16 [256, 4, 1024], P(('req', 'seq'))
- long_new_keys: bfloat16 [8, 4, 1024], P('req')
- long_new_values: bfloat16 [8, 4, 1024], P('req')
All inputs are finite; a program needn't handle non-finite values.
Results may differ from a plain program's by a relative error of at most 0.011.
Values may be sent and summed in bfloat16 or wider, within the bound.
No kernel may reach another device: no remote copies, remote signals or barrier semaphores. Data moves between devices by JAX's collectives and lax.ppermute only.
A program may use at most 128 MiB of HBM per device.

v0:
```python
import jax
import jax.numpy as jnp
from jax import lax
from jax.sharding import PartitionSpec as P

H = 16
HD = 64


masked_score = -1e30


def layer_norm(rows, gain):
    mean = jnp.mean(rows, axis=-1, keepdims=True)
    centred = rows - mean
    spread = jnp.mean(centred * centred, axis=-1, keepdims=True)
    return centred * lax.rsqrt(spread + 1e-05) * gain


def partial_block(query, keys, values, valid):
    scores = jnp.einsum("rhd,rphd->rhp", query, keys, preferred_element_type=jnp.float32) * 0.125
    window = valid[:, None, :]
    scores = jnp.where(window, scores, masked_score)
    peak = jnp.max(scores, axis=-1)
    weights = jnp.where(window, jnp.exp(scores - peak[..., None]), 0.0)
    total = jnp.sum(weights, axis=-1)
    output = jnp.einsum(
        "rhp,rphd->rhd", weights.astype(jnp.bfloat16), values, preferred_element_type=jnp.float32
    )
    return (peak, total, output)


def join(first, second):
    peak = jnp.maximum(first[0], second[0])
    scale_one = jnp.exp(first[0] - peak)
    scale_two = jnp.exp(second[0] - peak)
    total = first[1] * scale_one + second[1] * scale_two
    output = first[2] * scale_one[..., None] + second[2] * scale_two[..., None]
    return (peak, total, output)


def merge_long(partial_value):
    peak, total, output = partial_value
    top = lax.pmax(peak, "seq")
    scale = jnp.exp(peak - top)
    total_sum, output_sum = lax.psum((total * scale, output * scale[..., None]), "seq")
    return (top, total_sum, output_sum)


def shards(
    short_tokens,
    long_tokens,
    short_keys,
    short_values,
    long_keys,
    long_values,
    short_lengths,
    long_lengths,
    attn_gain,
    ffn_gain,
    w_query,
    w_key,
    w_value,
    w_out,
    w_up,
    w_down,
):
    short_count = short_tokens.shape[0]
    long_count = long_tokens.shape[0]
    steps = short_tokens.shape[1]
    width = short_tokens.shape[2]
    rows_count = short_count + long_count
    groups = lax.axis_size("req")
    block = long_keys.shape[1]
    anchor = lax.axis_index("seq") * block
    cache_short_k = short_keys.reshape(short_count, short_keys.shape[1], H, HD)
    cache_short_v = short_values.reshape(short_count, short_keys.shape[1], H, HD)
    cache_long_k = long_keys.reshape(long_count, block, H, HD)
    cache_long_v = long_values.reshape(long_count, block, H, HD)
    short_valid = jnp.arange(short_keys.shape[1])[None, :] < short_lengths[:, None]
    long_valid = (anchor + jnp.arange(block))[None, :] < long_lengths[:, None]
    stacked = jnp.concatenate([w_query, w_key, w_value], 1)
    local = w_query.shape[1]
    new_keys = jnp.zeros((rows_count, steps, width), jnp.bfloat16)
    new_values = jnp.zeros((rows_count, steps, width), jnp.bfloat16)
    fresh_ids = jnp.arange(steps)
    outputs = []
    for step in range(steps):
        rows = jnp.concatenate([short_tokens[:, step], long_tokens[:, step]], 0).astype(jnp.float32)
        normed = layer_norm(rows, attn_gain).astype(jnp.bfloat16)
        project_spread = jnp.dot(
            lax.all_gather(normed, "req", axis=0, tiled=True),
            stacked,
            preferred_element_type=jnp.float32,
        ).astype(jnp.bfloat16)
        moved = lax.all_to_all(project_spread, "req", split_axis=0, concat_axis=1, tiled=True)
        moved = moved.reshape(rows_count, groups, 3, local)
        query = moved[:, :, 0].reshape(rows_count, groups * local)
        key_now = moved[:, :, 1].reshape(rows_count, groups * local)
        value_now = moved[:, :, 2].reshape(rows_count, groups * local)
        query, key_now, value_now = (query, key_now, value_now)
        new_keys = new_keys.at[:, step].set(key_now)
        new_values = new_values.at[:, step].set(value_now)
        fresh_valid = jnp.broadcast_to(fresh_ids <= step, (rows_count, steps))
        queries = query.reshape(rows_count, H, HD)
        fresh_k = new_keys.reshape(rows_count, steps, H, HD)
        fresh_v = new_values.reshape(rows_count, steps, H, HD)
        fresh = partial_block(queries, fresh_k, fresh_v, fresh_valid)
        short_part = partial_block(queries[:short_count], cache_short_k, cache_short_v, short_valid)
        long_part = merge_long(
            partial_block(queries[short_count:], cache_long_k, cache_long_v, long_valid)
        )
        cache_part = jax.tree.map(
            lambda first, second: jnp.concatenate([first, second], 0), short_part, long_part
        )
        peak, total, output = join(cache_part, fresh)
        attended = (output / total[..., None]).reshape(rows_count, width).astype(jnp.bfloat16)
        spread = lax.all_to_all(attended, "req", split_axis=1, concat_axis=0, tiled=True)
        mixed = rows + lax.psum_scatter(
            jnp.dot(spread, w_out, preferred_element_type=jnp.float32),
            "req",
            scatter_dimension=0,
            tiled=True,
        )
        normed_ffn = layer_norm(mixed, ffn_gain).astype(jnp.bfloat16)
        hidden = jax.nn.gelu(
            jnp.dot(
                lax.all_gather(normed_ffn, "req", axis=0, tiled=True),
                w_up,
                preferred_element_type=jnp.float32,
            ),
            approximate=False,
        ).astype(jnp.bfloat16)
        result = mixed + lax.psum_scatter(
            jnp.dot(hidden, w_down, preferred_element_type=jnp.float32),
            "req",
            scatter_dimension=0,
            tiled=True,
        )
        outputs.append(result.astype(jnp.bfloat16))
    states = jnp.stack(outputs, axis=1)
    return (
        states[:short_count],
        states[short_count:],
        new_keys[:short_count],
        new_values[:short_count],
        new_keys[short_count:],
        new_values[short_count:],
    )


def solution(mesh):
    in_specs = (
        P(("req", "seq"), None, None),
        P("req", None, None),
        P(("req", "seq"), None, None),
        P(("req", "seq"), None, None),
        P("req", "seq", None),
        P("req", "seq", None),
        P(("req", "seq")),
        P("req"),
        P(),
        P(),
        P(None, "req"),
        P(None, "req"),
        P(None, "req"),
        P("req", None),
        P(None, "req"),
        P("req", None),
    )
    out_specs = (
        P(("req", "seq"), None, None),
        P("req", None, None),
        P(("req", "seq"), None, None),
        P(("req", "seq"), None, None),
        P("req", None, None),
        P("req", None, None),
    )
    return jax.shard_map(shards, mesh=mesh, in_specs=in_specs, out_specs=out_specs, check_vma=False)
```

profile of v0, /device:TPU:0, one launch (start us, length us, event | category | flops | bytes accessed | tf_op | source)
XLA Modules:
  0.0 525.6 jit_solution(3492423291342616036)
XLA Ops:
  7.2 1.0 fusion.459
  8.2 0.9 fusion.460
  11.3 13.2 %all-gather.6 = bf16[4,4,1024]{2,1,0:T(4,128)(2,1)S(1)} all-gather(bf16[1,4,1024]{2,1,0:T(4,128)(2,1)S(1)} %get-tuple-element.241), channel_id=1, replica_groups=mesh['req'=4,'seq'=32] {'req'}, dimensions={0}, use_global_device_ids=true | all-gather | bytes 40960 | tf_op jit(solution)/shard_map/all_gather | solution.py:92
  24.6 1.1 constant_dynamic-update-slice_fusion.2
  25.6 1.1 constant_dynamic-update-slice_fusion.1
  26.8 1.1 copy-done.2
  28.9 4.1 all-to-all-start.6
  33.1 12.8 %all-gather.4 = bf16[4,4,1024]{2,1,0:T(4,128)(2,1)S(1)} all-gather(bf16[1,4,1024]{2,1,0:T(4,128)(2,1)S(1)} %get-tuple-element.239), channel_id=1, replica_groups=mesh['req'=4,'seq'=32] {'req'}, dimensions={0}, use_global_device_ids=true | all-gather | bytes 40960 | tf_op jit(solution)/shard_map/all_gather | solution.py:92
  45.9 11.9 %all-gather.2 = bf16[4,4,1024]{2,1,0:T(4,128)(2,1)S(1)} all-gather(bf16[1,4,1024]{2,1,0:T(4,128)(2,1)S(1)} %get-tuple-element.240), channel_id=1, replica_groups=mesh['req'=4,'seq'=32] {'req'}, dimensions={0}, use_global_device_ids=true | all-gather | bytes 40960 | tf_op jit(solution)/shard_map/all_gather | solution.py:92
  57.9 11.9 %all-gather = bf16[4,4,1024]{2,1,0:T(4,128)(2,1)S(1)} all-gather(bf16[1,4,1024]{2,1,0:T(4,128)(2,1)S(1)} %get-tuple-element.242), channel_id=1, replica_groups=mesh['req'=4,'seq'=32] {'req'}, dimensions={0}, use_global_device_ids=true | all-gather | bytes 40960 | tf_op jit(solution)/shard_map/all_gather | solution.py:92
  69.9 1.8 convolution_convert_fusion.1
  71.7 1.7 convolution_convert_fusion.2
  73.8 1.5 copy.119
  75.3 2.3 copy.120
  79.5 6.2 %copy.117 = bf16[2,1024,1024]{1,2,0:T(8,128)(2,1)} copy(bf16[2,1024,1024]{2,1,0:T(8,128)(2,1)} %param.34) | data formatting | bytes 8388608 | tf_op args[2]
  85.7 6.2 %copy.118 = bf16[2,1024,1024]{1,2,0:T(8,128)(2,1)} copy(bf16[2,1024,1024]{2,1,0:T(8,128)(2,1)} %param.35) | data formatting | bytes 8388608 | tf_op args[3]
  91.9 3.6 all-to-all-start.4
  95.6 5.4 %all-to-all-done.4 = bf16[4,4,768]{2,1,0:T(4,128)(2,1)S(1)} async-done(((bf16[4,4,768]{2,1,0:T(4,128)(2,1)}), bf16[4,4,768]{2,1,0:T(4,128)(2,1)S(1)}, u32[]{:S(2)}, u32[]{:S(2)}) %all-to-all-start.4) | async-done | bytes 24608 | tf_op jit(solution)/shard_map/all_to_all | solution.py:96
  101.0 3.3 all-to-all-start.2
  104.3 5.3 %all-to-all-done.2 = bf16[4,4,768]{2,1,0:T(4,128)(2,1)S(1)} async-done(((bf16[4,4,768]{2,1,0:T(4,128)(2,1)}), bf16[4,4,768]{2,1,0:T(4,128)(2,1)S(1)}, u32[]{:S(2)}, u32[]{:S(2)}) %all-to-all-start.2) | async-done | bytes 24608 | tf_op jit(solution)/shard_map/all_to_all | solution.py:96
  109.6 3.3 all-to-all-start
  112.9 5.3 %all-to-all-done = bf16[4,4,768]{2,1,0:T(4,128)(2,1)S(1)} async-done(((bf16[4,4,768]{2,1,0:T(4,128)(2,1)}), bf16[4,4,768]{2,1,0:T(4,128)(2,1)S(1)}, u32[]{:S(2)}, u32[]{:S(2)}) %all-to-all-start) | async-done | bytes 24608 | tf_op jit(solution)/shard_map/all_to_all | solution.py:96
  120.1 62.9 %all-reduce.11 = (f32[2,16]{1,0:T(2,128)S(1)}, f32[2,16]{1,0:T(2,128)S(1)}, f32[2,16]{1,0:T(2,128)S(1)}, f32[2,16]{1,0:T(2,128)S(1)}) all-reduce(f32[2,16]{1,0:T(2,128)S(1)} %get-tuple-element.142, f32[2,16]{1,0:T(2,128)S(1)} %get-tuple-element.141, f32[2,16]{1,0:T(2,128)S(1)} %get-tuple-element.140, ...), channel_id=1, replica_groups=mesh['req'=4,'seq'=32] {'seq'}, use_global_device_ids=true, to_apply=%region_49.50 | all-reduce | flops 128 | bytes 1024 | tf_op jit(solution)/shard_map/pmax | solution.py:44
  183.4 1.6 fusion.110
  185.0 1.6 fusion.108
  191.7 3.0 fusion.478
  197.7 1.0 copy-done.5
  198.7 1.2 fusion.4
  199.9 1.2 fusion.6
  201.1 1.2 fusion.8
  202.3 1.2 fusion.10
  204.0 124.0 %all-reduce.10 = (f32[2,16,64]{2,1,0:T(8,128)S(1)}, f32[2,16]{1,0:T(2,128)S(1)}, f32[2,16,64]{2,1,0:T(8,128)S(1)}, f32[2,16]{1,0:T(2,128)S(1)}, f32[2,16,64]{2,1...) all-reduce(f32[2,16,64]{2,1,0:T(8,128)S(1)} %broadcast_multiply_fus, ...), channel_id=1, replica_groups=mesh['req'=4,'seq'=32] {'seq'}, use_global_device_ids=true, to_apply=%region_50.51 | all-reduce | flops 8320 | bytes 66560 | tf_op jit(solution)/shard_map/psum | solution.py:46
  328.8 3.2 all-to-all-start.7
  333.0 4.3 all-to-all-done.7
  337.3 3.2 all-to-all-start.5
  341.3 4.6 all-to-all-done.5
  345.9 3.2 all-to-all-start.3
  349.9 4.5 all-to-all-done.3
  354.4 3.2 all-to-all-start.1
  357.8 5.2 all-to-all-done.1
  363.8 0.8 fusion.474
  364.6 0.8 fusion.477
  367.5 35.5 %all-reduce.19.cloned.1.call-done = (f32[16,1024]{1,0:T(8,128)}, f32[16,1024]{1,0:T(8,128)}, f32[16,1024]{1,0:T(8,128)}, f32[16,1024]{1,0:T(8,128)}) async-done(((f32[16,1024]{1,0:T(8,128)}, f32[16,1024]{1,0:T(8,128)}, f32[16,1024]{1,0:T(8,128)}, f32[16,1024]{1,0:T(8,128)}), (f32[16,1024]{1,0:T(8,128)}, f32[16,1024]{1,0:T(8,128)}, f32[16,1024]{1,0:T(8,128)}, ...) | async-done | bytes 262160
  403.1 0.9 fusion.435
  404.0 0.9 multiply_reduce_fusion
  404.9 0.9 fusion.434
  405.8 0.9 multiply_reduce_fusion.1
  406.8 0.9 fusion.433
  407.7 0.9 multiply_reduce_fusion.2
  408.6 0.9 fusion.432
  409.5 0.9 multiply_reduce_fusion.3
  410.5 0.8 fusion.279
  411.3 0.9 fusion.276
  412.2 11.9 %all-gather.1 = bf16[4,4,1024]{2,1,0:T(4,128)(2,1)S(1)} all-gather(bf16[1,4,1024]{2,1,0:T(4,128)(2,1)S(1)} %get-tuple-element.236), channel_id=1, replica_groups=mesh['req'=4,'seq'=32] {'req'}, dimensions={0}, use_global_device_ids=true | all-gather | bytes 40960 | tf_op jit(solution)/shard_map/all_gather | solution.py:128
  424.2 12.1 %all-gather.7 = bf16[4,4,1024]{2,1,0:T(4,128)(2,1)S(1)} all-gather(bf16[1,4,1024]{2,1,0:T(4,128)(2,1)S(1)} %fusion.279), channel_id=1, replica_groups=mesh['req'=4,'seq'=32] {'req'}, dimensions={0}, use_global_device_ids=true | all-gather | bytes 40960 | tf_op jit(solution)/shard_map/all_gather | solution.py:128
  436.3 3.0 fusion.84
  439.3 3.0 fusion.90
  442.3 11.9 %all-gather.3 = bf16[4,4,1024]{2,1,0:T(4,128)(2,1)S(1)} all-gather(bf16[1,4,1024]{2,1,0:T(4,128)(2,1)S(1)} %get-tuple-element.237), channel_id=1, replica_groups=mesh['req'=4,'seq'=32] {'req'}, dimensions={0}, use_global_device_ids=true | all-gather | bytes 40960 | tf_op jit(solution)/shard_map/all_gather | solution.py:128
  454.3 3.0 fusion.88
  457.3 11.9 %all-gather.5 = bf16[4,4,1024]{2,1,0:T(4,128)(2,1)S(1)} all-gather(bf16[1,4,1024]{2,1,0:T(4,128)(2,1)S(1)} %get-tuple-element.238), channel_id=1, replica_groups=mesh['req'=4,'seq'=32] {'req'}, dimensions={0}, use_global_device_ids=true | all-gather | bytes 40960 | tf_op jit(solution)/shard_map/all_gather | solution.py:128
  469.2 3.0 fusion.86
  474.7 39.6 %all-reduce.17.cloned.1.call-done = (f32[16,1024]{1,0:T(8,128)}, f32[16,1024]{1,0:T(8,128)}, f32[16,1024]{1,0:T(8,128)}, f32[16,1024]{1,0:T(8,128)}) async-done(((f32[16,1024]{1,0:T(8,128)}, f32[16,1024]{1,0:T(8,128)}, f32[16,1024]{1,0:T(8,128)}, f32[16,1024]{1,0:T(8,128)}), (f32[16,1024]{1,0:T(8,128)}, f32[16,1024]{1,0:T(8,128)}, f32[16,1024]{1,0:T(8,128)}, ...) | async-done | bytes 262160
  515.1 0.8 fusion.281
  515.9 0.8 fusion.283
  (208 shorter events, 27.5 us)
Async XLA Ops:
  7.2 429.2 %copy-start = (bf16[1024,1024]{1,0:T(8,128)(2,1)S(1)}, bf16[1024,1024]{1,0:T(8,128)(2,1)}, u32[]{:S(2)}) copy-start(bf16[1024,1024]{1,0:T(8,128)(2,1)} %param.47) | copy-start | bytes 6291460
  7.2 19.6 %copy-start.7 = (bf16[1024,256]{1,0:T(8,128)(2,1)S(1)}, bf16[1024,256]{1,0:T(8,128)(2,1)}, u32[]{:S(2)}) copy-start(bf16[1024,256]{1,0:T(8,128)(2,1)} %param.44) | copy-start | bytes 1572868
  25.6 7.4 %copy-start.9 = (s32[2]{0:T(128)S(1)}, s32[2]{0:T(128)}, u32[]{:S(2)}) copy-start(s32[2]{0:T(128)} %param.38) | copy-start | bytes 28
  26.8 1.2 copy-start.2
  28.9 63.0 %all-to-all-start.6 = ((bf16[4,4,768]{2,1,0:T(4,128)(2,1)}), bf16[4,4,768]{2,1,0:T(4,128)(2,1)S(1)}, u32[]{:S(2)}, u32[]{:S(2)}) async-start(bf16[4,4,768]{2,1,0:T(4,128)(2,1)} %all_to_all.114), calls=%async_computation.6 | async-start | bytes 49152 | tf_op jit(solution)/shard_map/all_to_all | solution.py:96
  69.8 3.6 copy-start.3
  69.8 3.9 copy-start.10
  91.9 9.1 %all-to-all-start.4 = ((bf16[4,4,768]{2,1,0:T(4,128)(2,1)}), bf16[4,4,768]{2,1,0:T(4,128)(2,1)S(1)}, u32[]{:S(2)}, u32[]{:S(2)}) async-start(bf16[4,4,768]{2,1,0:T(4,128)(2,1)} %all_to_all.108), calls=%async_computation.4 | async-start | bytes 49152 | tf_op jit(solution)/shard_map/all_to_all | solution.py:96
  101.0 8.6 %all-to-all-start.2 = ((bf16[4,4,768]{2,1,0:T(4,128)(2,1)}), bf16[4,4,768]{2,1,0:T(4,128)(2,1)S(1)}, u32[]{:S(2)}, u32[]{:S(2)}) async-start(bf16[4,4,768]{2,1,0:T(4,128)(2,1)} %all_to_all.102), calls=%async_computation.2 | async-start | bytes 49152 | tf_op jit(solution)/shard_map/all_to_all | solution.py:96
  109.6 8.6 %all-to-all-start = ((bf16[4,4,768]{2,1,0:T(4,128)(2,1)}), bf16[4,4,768]{2,1,0:T(4,128)(2,1)S(1)}, u32[]{:S(2)}, u32[]{:S(2)}) async-start(bf16[4,4,768]{2,1,0:T(4,128)(2,1)} %all_to_all.96), calls=%async_computation | async-start | bytes 49152 | tf_op jit(solution)/shard_map/all_to_all | solution.py:96
  119.6 67.0 %copy-start.6 = (bf16[2,256,1024]{1,2,0:T(8,128)(2,1)S(1)}, bf16[2,256,1024]{1,2,0:T(8,128)(2,1)}, u32[]{:S(2)}) copy-start(bf16[2,256,1024]{1,2,0:T(8,128)(2,1)} %copy.120) | copy-start | bytes 3145732
  191.7 3.5 copy-start.1
  196.5 2.2 copy-start.5
  202.3 160.7 %copy-start.4 = (bf16[256,1024]{1,0:T(8,128)(2,1)S(1)}, bf16[256,1024]{1,0:T(8,128)(2,1)}, u32[]{:S(2)}) copy-start(bf16[256,1024]{1,0:T(8,128)(2,1)} %param.45) | copy-start | bytes 1572868
  203.5 162.8 %copy-start.11 = (u32[128]{0:T(128)S(1)}, u32[128]{0:T(128)}, u32[]{:S(2)}) copy-start(u32[128]{0:T(128)} %constant.304) | copy-start | bytes 1540
  203.5 207.0 %copy-start.8 = (f32[1024]{0:T(1024)S(1)}, f32[1024]{0:T(1024)}, u32[]{:S(2)}) copy-start(f32[1024]{0:T(1024)} %param.41) | copy-start | bytes 12292
  328.8 8.5 %all-to-all-start.7 = ((bf16[4,4,256]{2,0,1:T(4,128)(2,1)}), bf16[4,4,256]{2,0,1:T(4,128)(2,1)S(1)}, u32[]{:S(2)}, u32[]{:S(2)}) async-start(bf16[4,4,256]{2,0,1:T(4,128)(2,1)} %copy.133), calls=%async_computation.7 | async-start | bytes 16384 | tf_op jit(solution)/shard_map/all_to_all | solution.py:118
  337.3 8.5 %all-to-all-start.5 = ((bf16[4,4,256]{2,0,1:T(4,128)(2,1)}), bf16[4,4,256]{2,0,1:T(4,128)(2,1)S(1)}, u32[]{:S(2)}, u32[]{:S(2)}) async-start(bf16[4,4,256]{2,0,1:T(4,128)(2,1)} %copy.129), calls=%async_computation.5 | async-start | bytes 16384 | tf_op jit(solution)/shard_map/all_to_all | solution.py:118
  345.9 8.5 %all-to-all-start.3 = ((bf16[4,4,256]{2,0,1:T(4,128)(2,1)}), bf16[4,4,256]{2,0,1:T(4,128)(2,1)S(1)}, u32[]{:S(2)}, u32[]{:S(2)}) async-start(bf16[4,4,256]{2,0,1:T(4,128)(2,1)} %copy.125), calls=%async_computation.3 | async-start | bytes 16384 | tf_op jit(solution)/shard_map/all_to_all | solution.py:118
  354.4 8.5 %all-to-all-start.1 = ((bf16[4,4,256]{2,0,1:T(4,128)(2,1)}), bf16[4,4,256]{2,0,1:T(4,128)(2,1)S(1)}, u32[]{:S(2)}, u32[]{:S(2)}) async-start(bf16[4,4,256]{2,0,1:T(4,128)(2,1)} %copy.121), calls=%async_computation.1 | async-start | bytes 16384 | tf_op jit(solution)/shard_map/all_to_all | solution.py:118
  357.7 45.4 %all-reduce.19.cloned.1.call-start = ((), (), s32[]{:S(2)}) async-start(), calls=%async_computation.9 | async-start | bytes 524288
  366.2 148.1 %all-reduce.17.cloned.1.call-start = ((), (), s32[]{:S(2)}) async-start(), calls=%async_computation.8 | async-start | bytes 524288
Sparse Core Ops, SparseCore 0:
  366.3 36.6 all-reduce.18
  472.3 41.9 all-reduce.16
where the time goes:
time: 528 us; the launch traced here: 526 us
  blocking collectives  285 us (54%)
  waiting for transfers between devices  110 us (21%)
  local copies, waits for them, and re-layouts  35.8 us (7%)
  matrix products  35.8 us (7%)
  starting transfers between devices  27.4 us (5%)
  other arithmetic  17 us (3%)
  between operations  15.4 us (3%)
    psum x1, blocking collectives, merge_long(): lax.psum((total * scale, output * scale[..., None]), 'seq')  124 us
    unnamed x4, waiting for transfers between devices  75.1 us
    pmax x1, blocking collectives, merge_long(): top = lax.pmax(peak, 'seq')  62.9 us
    all_gather x4, blocking collectives, shards(): lax.all_gather(normed, 'req', axis=0, tiled=True)  49.9 us
    all_gather x4, blocking collectives, shards(): lax.all_gather(normed_ffn, 'req', axis=0, tiled=True)  47.9 us
    unnamed x53, local copies, waits for them, and re-layouts  25.4 us
    all_to_all x4, waiting for transfers between devices, shards(): lax.all_to_all(attended, 'req', split_axis=1, concat_axis=0, tiled=True)  18.6 us
    all_to_all x4, waiting for transfers between devices, shards(): lax.all_to_all(project_spread, 'req', split_axis=0, concat_axis=1, tiled=...  16 us
  transfers between devices with their start and end apart: 10, of which 9 were waited for; matrix products, arithmetic and copies ran while one was open for 5% of the time, Pallas kernels for 0%

commit v1 on v0

v1 whole, which is shorter than its diff:
```python
import jax
import jax.numpy as jnp
from jax import lax
from jax.sharding import PartitionSpec as P

H = 16
HD = 64


masked_score = -1e30


def layer_norm(rows, gain):
    mean = jnp.mean(rows, axis=-1, keepdims=True)
    centred = rows - mean
    spread = jnp.mean(centred * centred, axis=-1, keepdims=True)
    return centred * lax.rsqrt(spread + 1e-05) * gain


def partial_block(query, keys, values, valid):
    scores = jnp.einsum("rthd,rphd->rhtp", query, keys, preferred_element_type=jnp.float32) * 0.125
    scores = jnp.where(valid, scores, masked_score)
    peak = jnp.max(scores, axis=-1)
    weights = jnp.where(valid, jnp.exp(scores - peak[..., None]), 0.0)
    total = jnp.sum(weights, axis=-1)
    output = jnp.einsum(
        "rhtp,rphd->rhtd", weights.astype(jnp.bfloat16), values, preferred_element_type=jnp.float32
    )
    return (peak, total, output)


def join(first, second):
    peak = jnp.maximum(first[0], second[0])
    scale_one = jnp.exp(first[0] - peak)
    scale_two = jnp.exp(second[0] - peak)
    total = first[1] * scale_one + second[1] * scale_two
    output = first[2] * scale_one[..., None] + second[2] * scale_two[..., None]
    return (peak, total, output)


def merge_long(partial_value):
    peak, total, output = partial_value
    top = lax.pmax(peak, "seq")
    scale = jnp.exp(peak - top)
    total_sum, output_sum = lax.psum((total * scale, output * scale[..., None]), "seq")
    return (top, total_sum, output_sum)


def shards(
    short_tokens,
    long_tokens,
    short_keys,
    short_values,
    long_keys,
    long_values,
    short_lengths,
    long_lengths,
    attn_gain,
    ffn_gain,
    w_query,
    w_key,
    w_value,
    w_out,
    w_up,
    w_down,
):
    short_count = short_tokens.shape[0]
    long_count = long_tokens.shape[0]
    steps = short_tokens.shape[1]
    width = short_tokens.shape[2]
    req_count = short_count + long_count
    rows_count = req_count * steps
    groups = lax.axis_size("req")
    block = long_keys.shape[1]
    anchor = lax.axis_index("seq") * block
    cache_short_k = short_keys.reshape(short_count, short_keys.shape[1], H, HD)
    cache_short_v = short_values.reshape(short_count, short_keys.shape[1], H, HD)
    cache_long_k = long_keys.reshape(long_count, block, H, HD)
    cache_long_v = long_values.reshape(long_count, block, H, HD)
    short_valid = (jnp.arange(short_keys.shape[1])[None, :] < short_lengths[:, None])[:, None, None, :]
    long_valid = ((anchor + jnp.arange(block))[None, :] < long_lengths[:, None])[:, None, None, :]
    stacked = jnp.concatenate([w_query, w_key, w_value], 1)
    local = w_query.shape[1]
    fresh_ids = jnp.arange(steps)
    fresh_valid = (fresh_ids[None, :] <= fresh_ids[:, None])[None, None, :, :]

    rows = jnp.concatenate([short_tokens, long_tokens], 0).reshape(rows_count, width).astype(jnp.float32)
    normed = layer_norm(rows, attn_gain).astype(jnp.bfloat16)
    project_spread = jnp.dot(
        lax.all_gather(normed, "req", axis=0, tiled=True),
        stacked,
        preferred_element_type=jnp.float32,
    ).astype(jnp.bfloat16)
    moved = lax.all_to_all(project_spread, "req", split_axis=0, concat_axis=1, tiled=True)
    moved = moved.reshape(rows_count, groups, 3, local)
    query = moved[:, :, 0].reshape(req_count, steps, H, HD)
    key_now = moved[:, :, 1].reshape(req_count, steps, width)
    value_now = moved[:, :, 2].reshape(req_count, steps, width)
    fresh_k = key_now.reshape(req_count, steps, H, HD)
    fresh_v = value_now.reshape(req_count, steps, H, HD)
    fresh = partial_block(query, fresh_k, fresh_v, fresh_valid)
    short_part = partial_block(query[:short_count], cache_short_k, cache_short_v, short_valid)
    long_part = merge_long(
        partial_block(query[short_count:], cache_long_k, cache_long_v, long_valid)
    )
    cache_part = jax.tree.map(
        lambda first, second: jnp.concatenate([first, second], 0), short_part, long_part
    )
    peak, total, output = join(cache_part, fresh)
    attended = output / total[..., None]
    attended = attended.transpose(0, 2, 1, 3).reshape(rows_count, width).astype(jnp.bfloat16)
    spread = lax.all_to_all(attended, "req", split_axis=1, concat_axis=0, tiled=True)
    mixed = rows + lax.psum_scatter(
        jnp.dot(spread, w_out, preferred_element_type=jnp.float32),
        "req",
        scatter_dimension=0,
        tiled=True,
    )
    normed_ffn = layer_norm(mixed, ffn_gain).astype(jnp.bfloat16)
    hidden = jax.nn.gelu(
        jnp.dot(
            lax.all_gather(normed_ffn, "req", axis=0, tiled=True),
            w_up,
            preferred_element_type=jnp.float32,
        ),
        approximate=False,
    ).astype(jnp.bfloat16)
    result = mixed + lax.psum_scatter(
        jnp.dot(hidden, w_down, preferred_element_type=jnp.float32),
        "req",
        scatter_dimension=0,
        tiled=True,
    )
    states = result.astype(jnp.bfloat16).reshape(req_count, steps, width)
    return (
        states[:short_count],
        states[short_count:],
        key_now[:short_count],
        value_now[:short_count],
        key_now[short_count:],
        value_now[short_count:],
    )


def solution(mesh):
    in_specs = (
        P(("req", "seq"), None, None),
        P("req", None, None),
        P(("req", "seq"), None, None),
        P(("req", "seq"), None, None),
        P("req", "seq", None),
        P("req", "seq", None),
        P(("req", "seq")),
        P("req"),
        P(),
        P(),
        P(None, "req"),
        P(None, "req"),
        P(None, "req"),
        P("req", None),
        P(None, "req"),
        P("req", None),
    )
    out_specs = (
        P(("req", "seq"), None, None),
        P("req", None, None),
        P(("req", "seq"), None, None),
        P(("req", "seq"), None, None),
        P("req", None, None),
        P("req", None, None),
    )
    return jax.shard_map(shards, mesh=mesh, in_specs=in_specs, out_specs=out_specs, check_vma=False)
```

time: 528 us -> 384 us (0.73)
  waiting for transfers between devices: 110 us -> 34 us
  starting transfers between devices: 27.4 us -> 4.3 us
  matrix products: 35.8 us -> 13.4 us
  other arithmetic: 17 us -> 6.54 us
  local copies, waits for them, and re-layouts: 35.8 us -> 26 us
    unnamed x4 -> x2, waiting for transfers between devices: 75.1 us -> 0.03 us
    pmax x1, blocking collectives: 62.9 us -> 125 us  [merge_long(): top = lax.pmax(peak, 'seq')]
    all_gather x4 -> x1, blocking collectives: 49.9 us -> 13.3 us  [shards(): lax.all_gather(normed, 'req', axis=0, tiled=True)]
    all_gather x4 -> x1, blocking collectives: 47.9 us -> 12 us  [shards(): lax.all_gather(normed_ffn, 'req', axis=0, tiled=True)]
    reduce_scatter x0 -> x2, waiting for transfers between devices: none -> 34 us  [the longest x1 18.3 us: shards(): lax.psum_scatter(jnp.dot(hidden, w_down, preferred_element_type=jnp.float...]
    all_to_all x4 -> x0, waiting for transfers between devices: 18.6 us -> none  [shards(): lax.all_to_all(attended, 'req', split_axis=1, concat_axis=0, tiled=True)]
    all_to_all x4 -> x1, waiting for transfers between devices: 16 us -> 0.01 us  [shards(): lax.all_to_all(project_spread, 'req', split_axis=0, concat_axis=1, tiled=...]
    all_to_all x4 -> x0, starting transfers between devices: 13 us -> none  [shards(): lax.all_to_all(attended, 'req', split_axis=1, concat_axis=0, tiled=True)]
  transfers between devices with their start and end apart: 10 -> 3, of which waited for: 9 -> 2; matrix products, arithmetic and copies ran while one was open for 5% -> 5% of each run, Pallas kernels for 0% -> 0%
where the time goes in v1:
time: 384 us; the launch traced here: 382 us
  blocking collectives  284 us (74%)
  waiting for transfers between devices  34 us (9%)
  local copies, waits for them, and re-layouts  26 us (7%)
  between operations  14.3 us (4%)
  matrix products  13.4 us (3%)
  other arithmetic  6.54 us (2%)
  starting transfers between devices  4.3 us (1%)
    pmax x1, blocking collectives, merge_long(): top = lax.pmax(peak, 'seq')  125 us
    psum x1, blocking collectives, merge_long(): lax.psum((total * scale, output * scale[..., None]), 'seq')  124 us
    reduce_scatter x1, waiting for transfers between devices, shards(): lax.psum_scatter(jnp.dot(hidden, w_down, preferred_element_type=jnp.float...  18.3 us
    unnamed x32, local copies, waits for them, and re-layouts  16.5 us
    reduce_scatter x1, waiting for transfers between devices, shards(): lax.psum_scatter(jnp.dot(spread, w_out, preferred_element_type=jnp.float3...  15.6 us
    all_gather x1, blocking collectives, shards(): lax.all_gather(normed, 'req', axis=0, tiled=True)  13.3 us
    all_gather x1, blocking collectives, shards(): lax.all_gather(normed_ffn, 'req', axis=0, tiled=True)  12 us
    all_to_all x1, blocking collectives, shards(): lax.all_to_all(attended, 'req', split_axis=1, concat_axis=0, tiled=True)  9.76 us
  transfers between devices with their start and end apart: 3, of which 2 were waited for; matrix products, arithmetic and copies ran while one was open for 5% of the time, Pallas kernels for 0%

profile of v1, /device:TPU:0, one launch (start us, length us, event | category | flops | bytes accessed | tf_op | source)
XLA Modules:
  0.0 382.5 jit_solution(11535167643442120678)
XLA Ops:
  7.2 0.0 copy-start
  7.2 1.0 fusion.115
  8.2 0.1 div.23
  8.3 0.9 multiply_reduce_fusion.1
  9.2 0.8 maximum_convert_fusion
  10.0 0.1 rsqrt.20
  10.1 0.8 multiply_convert_fusion.1
  10.8 13.3 %all_gather.6 = bf16[64,1024]{1,0:T(8,128)(2,1)S(1)} all-gather(bf16[16,1024]{1,0:T(8,128)(2,1)S(1)} %multiply_convert_fusion.1), channel_id=1, replica_groups=mesh['req'=4,'seq'=32] {'req'}, dimensions={0}, use_global_device_ids=true | all-gather | bytes 163840 | tf_op jit(solution)/shard_map/all_gather | solution.py:90
  24.2 2.4 fusion.7
  26.5 4.3 %all-to-all-start = ((bf16[4,16,768]{2,1,0:T(8,128)(2,1)}), bf16[4,16,768]{2,1,0:T(8,128)(2,1)S(1)}, u32[]{:S(2)}, u32[]{:S(2)}) async-start(bf16[4,16,768]{2,1,0:T(8,128)(2,1)} %bitcast), calls=%async_computation | async-start | bytes 196608 | tf_op jit(solution)/shard_map/all_to_all | solution.py:94
  30.8 0.1 iota_compare_fusion
  30.9 1.5 copy.151
  32.4 2.3 copy.153
  34.7 6.2 %copy.147 = bf16[2,1024,1024]{1,2,0:T(8,128)(2,1)} copy(bf16[2,1024,1024]{2,1,0:T(8,128)(2,1)} %param.18) | data formatting | bytes 8388608 | tf_op args[2]
  40.9 6.2 %copy.149 = bf16[2,1024,1024]{1,2,0:T(8,128)(2,1)} copy(bf16[2,1024,1024]{2,1,0:T(8,128)(2,1)} %param.19) | data formatting | bytes 8388608 | tf_op args[3]
  47.1 0.1 broadcast_compare_fusion
  47.2 0.0 all-to-all-done
  47.3 0.8 fusion.120
  48.1 0.1 fusion.121
  48.3 0.1 reshape_reshape_squeeze.6
  48.4 0.7 reshape_squeeze.2
  49.2 1.0 fusion.68
  50.2 0.2 copy.158
  50.4 0.1 fusion.79
  50.5 0.1 fusion.80
  50.6 0.1 copy.171
  50.7 0.8 copy.150
  51.5 0.1 slice.66
  51.6 0.8 copy.146
  52.4 0.1 slice.64
  52.5 0.7 reshape_reshape_squeeze.7
  53.2 0.1 copy.172
  53.3 0.8 copy.162
  54.1 0.3 fusion.123
  54.5 125.1 %pmax.7 = f32[2,16,4]{2,1,0:T(8,128)S(1)} all-reduce(f32[2,16,4]{2,1,0:T(8,128)S(1)} %get-tuple-element.28), channel_id=1, replica_groups=mesh['req'=4,'seq'=32] {'seq'}, use_global_device_ids=true, to_apply=%region_4.5 | all-reduce | flops 128 | bytes 1024 | tf_op jit(solution)/shard_map/pmax | solution.py:43
  179.5 0.2 fusion.64
  179.7 3.1 fusion.124
  182.8 0.4 fusion.15
  183.2 1.2 fusion.17
  184.5 0.4 convolution_multiply_fusion.3
  184.9 123.9 %all-reduce = (f32[2,16,4,64]{3,2,1,0:T(4,128)S(1)}, f32[2,16,4]{2,1,0:T(8,128)S(1)}) all-reduce(f32[2,16,4,64]{3,2,1,0:T(4,128)S(1)} %convolution_multiply_fusion.3, f32[2,16,4]{2,1,0:T(8,128)S(1)} %get-tuple-element.13), channel_id=1, replica_groups=mesh['req'=4,'seq'=32] {'seq'}, use_global_device_ids=true, to_apply=%region_5.6 | all-reduce | flops 8320 | bytes 66560 | tf_op jit(solution)/shard_map/psum | solution.py:45
  308.8 0.0 copy-done.8
  308.8 0.0 copy-done.9
  308.8 0.3 fusion.14
  309.1 0.1 convert_element_type.54
  309.3 9.8 %all_to_all.32 = bf16[16,4,256]{2,0,1:T(8,128)(2,1)S(1)} all-to-all(bf16[16,4,256]{2,0,1:T(8,128)(2,1)S(1)} %copy.166), channel_id=1, replica_groups=mesh['req'=4,'seq'=32] {'req'}, dimensions={1} | all-to-all | bytes 65536 | tf_op jit(solution)/shard_map/all_to_all | solution.py:112
  319.0 0.9 fusion.127
  319.9 0.0 reduce-scatter.3.cloned.1.call-update
  320.0 0.0 reduce-scatter.5.cloned.1.call-start
  320.0 15.6 %reduce-scatter.3.cloned.1.call-done = f32[16,1024]{1,0:T(8,128)} async-done(((f32[64,1024]{1,0:T(8,128)}), f32[16,1024]{1,0:T(8,128)}) %reduce-scatter.3.cloned.1.call-update) | async-done | bytes 65552 | tf_op jit(solution)/shard_map/reduce_scatter | solution.py:113
  335.6 1.0 fusion.116
  336.6 0.2 multiply_reduce_fusion
  336.8 0.1 multiply_convert_fusion
  336.9 12.0 %all_gather.7 = bf16[64,1024]{1,0:T(8,128)(2,1)S(1)} all-gather(bf16[16,1024]{1,0:T(8,128)(2,1)S(1)} %multiply_convert_fusion), channel_id=1, replica_groups=mesh['req'=4,'seq'=32] {'req'}, dimensions={0}, use_global_device_ids=true | all-gather | bytes 163840 | tf_op jit(solution)/shard_map/all_gather | solution.py:122
  348.9 3.7 fusion.32
  352.6 0.0 reduce-scatter.5.cloned.1.call-update
  352.7 0.6 slice.81
  353.3 0.6 slice.79
  354.0 0.6 slice.77
  354.6 0.6 slice.75
  355.2 18.3 %reduce-scatter.5.cloned.1.call-done = f32[16,1024]{1,0:T(8,128)} async-done(((f32[64,1024]{1,0:T(8,128)}), f32[16,1024]{1,0:T(8,128)}) %reduce-scatter.5.cloned.1.call-update) | async-done | bytes 65552 | tf_op jit(solution)/shard_map/reduce_scatter | solution.py:128
  373.6 0.8 add_convert_fusion
  374.4 0.6 slice.73
  375.0 0.6 slice.71
  (44 shorter events, 0.4 us)
Async XLA Ops:
  7.2 341.7 %copy-start = (bf16[1024,1024]{1,0:T(8,128)(2,1)S(1)}, bf16[1024,1024]{1,0:T(8,128)(2,1)}, u32[]{:S(2)}) copy-start(bf16[1024,1024]{1,0:T(8,128)(2,1)} %param.31) | copy-start | bytes 6291460
  7.2 23.6 %copy-start.11 = (s32[2]{0:T(128)S(1)}, s32[2]{0:T(128)}, u32[]{:S(2)}) copy-start(s32[2]{0:T(128)} %param.22) | copy-start | bytes 28
  26.5 20.7 %all-to-all-start = ((bf16[4,16,768]{2,1,0:T(8,128)(2,1)}), bf16[4,16,768]{2,1,0:T(8,128)(2,1)S(1)}, u32[]{:S(2)}, u32[]{:S(2)}) async-start(bf16[4,16,768]{2,1,0:T(8,128)(2,1)} %bitcast), calls=%async_computation | async-start | bytes 196608 | tf_op jit(solution)/shard_map/all_to_all | solution.py:94
  30.8 304.9 %reduce-scatter.3.cloned.1.call-start = ((), (), s32[]{:S(2)}) async-start(), calls=%async_computation.4 | async-start | bytes 327680 | tf_op jit(solution)/shard_map/reduce_scatter | solution.py:113
  40.9 6.2 %copy-start.12 = (s32[2]{0:T(128)S(1)}, s32[2]{0:T(128)}, u32[]{:S(2)}) copy-start(s32[2]{0:T(128)} %param.23) | copy-start | bytes 28
  179.5 3.7 copy-start.1
  182.8 1.7 copy-start.2
  183.2 125.6 %copy-start.8 = (bf16[4,16,4,4]{3,2,1,0:T(4,128)(2,1)S(1)}, bf16[4,16,4,4]{3,2,1,0:T(4,128)(2,1)}, u32[]{:S(2)}) copy-start(bf16[4,16,4,4]{3,2,1,0:T(4,128)(2,1)} %copy.162) | copy-start | bytes 6148
  183.2 125.6 %copy-start.9 = (bf16[4,4,16,64]{3,2,1,0:T(8,128)(2,1)S(1)}, bf16[4,4,16,64]{3,2,1,0:T(8,128)(2,1)}, u32[]{:S(2)}) copy-start(bf16[4,4,16,64]{3,2,1,0:T(8,128)(2,1)} %reshape_reshape_squeeze.7) | copy-start | bytes 98308
  184.4 134.6 %copy-start.3 = (bf16[256,1024]{1,0:T(8,128)(2,1)S(1)}, bf16[256,1024]{1,0:T(8,128)(2,1)}, u32[]{:S(2)}) copy-start(bf16[256,1024]{1,0:T(8,128)(2,1)} %param.29) | copy-start | bytes 1572868
  184.4 152.4 %copy-start.10 = (f32[1024]{0:T(1024)S(1)}, f32[1024]{0:T(1024)}, u32[]{:S(2)}) copy-start(f32[1024]{0:T(1024)} %param.25) | copy-start | bytes 12292
  320.0 53.6 %reduce-scatter.5.cloned.1.call-start = ((), (), s32[]{:S(2)}) async-start(), calls=%async_computation.5 | async-start | bytes 327680 | tf_op jit(solution)/shard_map/reduce_scatter | solution.py:128
  348.9 3.8 copy-start.7
  348.9 4.4 %copy-start.6 = (bf16[8,4,1,256]{3,2,0,1:T(2,128)(2,1)S(1)}, bf16[8,4,1,256]{3,2,0,1:T(2,128)(2,1)}, u32[]{:S(2)}) copy-start(bf16[8,4,1,256]{3,2,0,1:T(2,128)(2,1)} %get-tuple-element.16) | copy-start | bytes 49156
  348.9 5.0 %copy-start.5 = (bf16[8,4,1,256]{3,2,0,1:T(2,128)(2,1)S(1)}, bf16[8,4,1,256]{3,2,0,1:T(2,128)(2,1)}, u32[]{:S(2)}) copy-start(bf16[8,4,1,256]{3,2,0,1:T(2,128)(2,1)} %get-tuple-element.17) | copy-start | bytes 49156
  348.9 5.7 %copy-start.4 = (bf16[8,4,1,256]{3,2,0,1:T(2,128)(2,1)S(1)}, bf16[8,4,1,256]{3,2,0,1:T(2,128)(2,1)}, u32[]{:S(2)}) copy-start(bf16[8,4,1,256]{3,2,0,1:T(2,128)(2,1)} %get-tuple-element.18) | copy-start | bytes 49156
Sparse Core Ops, SparseCore 0:
  320.1 15.5 reduce-scatter.2
  352.8 20.7 reduce-scatter.4

commit v2 on v1

--- a/solution.py
+++ b/solution.py
@@ -40,10 +40,25 @@
 
 def merge_long(partial_value):
     peak, total, output = partial_value
-    top = lax.pmax(peak, "seq")
-    scale = jnp.exp(peak - top)
-    total_sum, output_sum = lax.psum((total * scale, output * scale[..., None]), "seq")
-    return (top, total_sum, output_sum)
+    packed = jnp.concatenate([output, peak[..., None], total[..., None]], -1)
+    size = lax.axis_size("seq")
+    me = lax.axis_index("seq")
+    width = output.shape[-1]
+    distance = 1
+    while distance < size:
+        pairs = [(i, i ^ distance) for i in range(size)]
+        other = lax.ppermute(packed, "seq", pairs)
+        lower = (me & distance) == 0
+        first = jnp.where(lower, packed, other)
+        second = jnp.where(lower, other, packed)
+        top = jnp.maximum(first[..., width], second[..., width])
+        scale_one = jnp.exp(first[..., width] - top)[..., None]
+        scale_two = jnp.exp(second[..., width] - top)[..., None]
+        merged = first[..., :width] * scale_one + second[..., :width] * scale_two
+        summed = first[..., width + 1:] * scale_one + second[..., width + 1:] * scale_two
+        packed = jnp.concatenate([merged, top[..., None], summed], -1)
+        distance *= 2
+    return (packed[..., width], packed[..., width + 1], packed[..., :width])
 
 
 def shards(

time: 384 us -> 185 us (0.48)
  blocking collectives: 284 us -> 35.4 us
  waiting for transfers between devices: 34 us -> 56.2 us
  other arithmetic: 6.54 us -> 16.3 us
  starting transfers between devices: 4.3 us -> 14 us
  local copies, waits for them, and re-layouts: 26 us -> 30 us
    pmax x1 -> x0, blocking collectives: 125 us -> none  [merge_long(): top = lax.pmax(peak, 'seq')]
    psum x1 -> x0, blocking collectives: 124 us -> none  [merge_long(): lax.psum((total * scale, output * scale[..., None]), 'seq')]
    ppermute x0 -> x5, waiting for transfers between devices: none -> 17.2 us  [merge_long(): other = lax.ppermute(packed, 'seq', pairs)]
    ppermute x0 -> x5, starting transfers between devices: none -> 9.68 us  [merge_long(): other = lax.ppermute(packed, 'seq', pairs)]
    reduce_scatter x1, waiting for transfers between devices: 15.6 us -> 20.7 us  [shards(): lax.psum_scatter(jnp.dot(spread, w_out, preferred_element_type=jnp.float3...]
    unnamed x32 -> x38, local copies, waits for them, and re-layouts: 16.5 us -> 17.1 us
  transfers between devices with their start and end apart: 3 -> 8, of which waited for: 2 -> 6; matrix products, arithmetic and copies ran while one was open for 5% -> 18% of each run, Pallas kernels for 0% -> 0%
where the time goes in v2:
time: 185 us; the launch traced here: 183 us
  waiting for transfers between devices  56.2 us (30%)
  blocking collectives  35.4 us (19%)
  local copies, waits for them, and re-layouts  30 us (16%)
  matrix products  17 us (9%)
  other arithmetic  16.3 us (9%)
  between operations  14.5 us (8%)
  starting transfers between devices  14 us (8%)
    reduce_scatter x1, waiting for transfers between devices, shards(): lax.psum_scatter(jnp.dot(spread, w_out, preferred_element_type=jnp.float3...  20.7 us
    reduce_scatter x1, waiting for transfers between devices, shards(): lax.psum_scatter(jnp.dot(hidden, w_down, preferred_element_type=jnp.float...  18.3 us
    ppermute x5, waiting for transfers between devices, merge_long(): other = lax.ppermute(packed, 'seq', pairs)  17.2 us
    unnamed x38, local copies, waits for them, and re-layouts  17.1 us
    all_gather x1, blocking collectives, shards(): lax.all_gather(normed, 'req', axis=0, tiled=True)  13.3 us
    all_gather x1, blocking collectives, shards(): lax.all_gather(normed_ffn, 'req', axis=0, tiled=True)  12 us
    all_to_all x1, blocking collectives, shards(): lax.all_to_all(attended, 'req', split_axis=1, concat_axis=0, tiled=True)  10.1 us
    ppermute x5, starting transfers between devices, merge_long(): other = lax.ppermute(packed, 'seq', pairs)  9.68 us
  transfers between devices with their start and end apart: 8, of which 6 were waited for; matrix products, arithmetic and copies ran while one was open for 18% of the time, Pallas kernels for 0%

profile of v2, /device:TPU:0, one launch (start us, length us, event | category | flops | bytes accessed | tf_op | source)
XLA Modules:
  0.0 183.3 jit_solution(8223218996991760599)
XLA Ops:
  7.2 1.0 fusion.138
  8.3 0.9 multiply_reduce_fusion.1
  9.2 0.8 maximum_convert_fusion
  10.1 0.8 multiply_convert_fusion.1
  10.9 13.3 %all_gather.6 = bf16[64,1024]{1,0:T(8,128)(2,1)S(1)} all-gather(bf16[16,1024]{1,0:T(8,128)(2,1)S(1)} %multiply_convert_fusion.1), channel_id=1, replica_groups=mesh['req'=4,'seq'=32] {'req'}, dimensions={0}, use_global_device_ids=true | all-gather | bytes 163840 | tf_op jit(solution)/shard_map/all_gather | solution.py:105
  24.2 2.4 %fusion.7 = bf16[64,768]{1,0:T(8,128)(2,1)} fusion(bf16[64,1024]{1,0:T(8,128)(2,1)S(1)} %all_gather.6, bf16[1024,256]{1,0:T(8,128)(2,1)} %param.28, bf16[1024,256]{1,0:T(8,128)(2,1)} %param.27, bf16[1024,256]{1,0:T(8,128)(2,1)} %param.26), kind=kOutput, calls=%fused_computation.8 | convolution fusion | flops 105431040 | bytes 1802240 | tf_op jit(solution)/shard_map/dot_general | solution.py:104
  26.5 4.3 %all-to-all-start = ((bf16[4,16,768]{2,1,0:T(8,128)(2,1)}), bf16[4,16,768]{2,1,0:T(8,128)(2,1)S(1)}, u32[]{:S(2)}, u32[]{:S(2)}) async-start(bf16[4,16,768]{2,1,0:T(8,128)(2,1)} %bitcast.75), calls=%async_computation | async-start | bytes 196608 | tf_op jit(solution)/shard_map/all_to_all | solution.py:109
  30.8 0.7 iota_compare_fusion
  31.5 1.4 copy.411
  32.8 1.5 copy.413
  34.3 6.2 %copy.407 = bf16[2,1024,1024]{1,2,0:T(8,128)(2,1)} copy(bf16[2,1024,1024]{2,1,0:T(8,128)(2,1)} %param.18) | data formatting | bytes 8388608 | tf_op args[2]
  40.6 6.3 %copy.409 = bf16[2,1024,1024]{1,2,0:T(8,128)(2,1)} copy(bf16[2,1024,1024]{2,1,0:T(8,128)(2,1)} %param.19) | data formatting | bytes 8388608 | tf_op args[3]
  46.8 0.6 broadcast_compare_fusion
  47.5 0.5 iota_compare_fusion.1
  48.0 0.8 fusion.142
  49.1 0.7 slice.166
  49.8 0.8 copy.406
  50.5 0.7 slice.164
  51.3 0.7 reshape_reshape_squeeze.6
  52.1 0.7 reshape_squeeze.2
  52.8 1.6 fusion.145
  54.5 0.9 fusion.69
  55.4 1.1 fusion.71
  56.9 3.1 %fusion.146 = (f32[2,16,4]{2,1,0:T(8,128)S(1)}, f32[2,16,4,1024]{3,2,1,0:T(4,128)S(1)}) fusion(bf16[2,1024,16,64]{1,3,2,0:T(8,128)(2,1)} %bitcast.70, bf16[2,4,16,64]{3,2,1,0:T(8,128)(2,1)S(1)} %copy-done.3, pred[2,1024]{1,0:T(4,128)(4,1)} %iota_compare_fusion), kind=kOutput, calls=%fused_computation.223 | convolution fusion | flops 17170304 | bytes 4737536 | tf_op jit(solution)/shard_map/rthd,rphd->rhtp/dot_general | solution.py:21
  60.0 0.2 copy-done.1
  60.2 1.2 fusion.16
  61.4 0.9 fusion.75
  62.3 1.1 copy.423
  63.4 1.1 broadcast_select_fusion.1
  64.7 1.7 collective-permute-start.1
  66.5 6.9 %collective-permute-done.1 = f32[2,16,4,66]{1,2,3,0:T(4,128)S(1)} collective-permute-done((f32[2,16,4,66]{1,2,3,0:T(4,128)S(1)}, f32[2,16,4,66]{1,2,3,0:T(4,128)S(1)}, u32[]{:S(2)}, u32[]{:S(2)}) %collective-permute-start.1) | collective-permute-done | bytes 33824 | tf_op jit(solution)/shard_map/ppermute | solution.py:50
  73.7 3.3 %collective-permute-start.2 = (f32[2,16,4,66]{1,2,3,0:T(4,128)S(1)}, f32[2,16,4,66]{1,2,3,0:T(4,128)}, u32[]{:S(2)}, u32[]{:S(2)}) collective-permute-start(f32[2,16,4,66]{1,2,3,0:T(4,128)S(1)} %pad_maximum_fusion.2), channel_id=1, source_target_pairs={{0,4},{1,5},{2,6},{3,7},{4,0},{5,1},{6,2},{7,3},{8,12},{9,13},{10,... | collective-permute-start | bytes 101384 | tf_op jit(solution)/shard_map/ppermute | solution.py:50
  76.9 0.7 fusion.88
  77.7 0.7 reshape_reshape_squeeze.7
  78.4 0.2 copy.428
  78.6 4.4 %collective-permute-done.2 = f32[2,16,4,66]{1,2,3,0:T(4,128)} collective-permute-done((f32[2,16,4,66]{1,2,3,0:T(4,128)S(1)}, f32[2,16,4,66]{1,2,3,0:T(4,128)}, u32[]{:S(2)}, u32[]{:S(2)}) %collective-permute-start.2) | collective-permute-done | bytes 33824 | tf_op jit(solution)/shard_map/ppermute | solution.py:50
  83.0 1.1 broadcast_select_fusion.5
  84.3 1.6 collective-permute-start.3
  85.9 1.0 fusion.73
  86.9 4.3 %collective-permute-done.3 = f32[2,16,4,66]{1,2,3,0:T(4,128)S(1)} collective-permute-done((f32[2,16,4,66]{1,2,3,0:T(4,128)S(1)}, f32[2,16,4,66]{1,2,3,0:T(4,128)S(1)}, u32[]{:S(2)}, u32[]{:S(2)}) %collective-permute-start.3) | collective-permute-done | bytes 33824 | tf_op jit(solution)/shard_map/ppermute | solution.py:50
  91.6 3.1 %collective-permute-start.4 = (f32[2,16,4,66]{1,2,3,0:T(4,128)S(1)}, f32[2,16,4,66]{1,2,3,0:T(4,128)}, u32[]{:S(2)}, u32[]{:S(2)}) collective-permute-start(f32[2,16,4,66]{1,2,3,0:T(4,128)S(1)} %pad_maximum_fusion.4), channel_id=1, source_target_pairs={{0,16},{1,17},{2,18},{3,19},{4,20},{5,21},{6,22},{7,23},{8,24},{9,... | collective-permute-start | bytes 101384 | tf_op jit(solution)/shard_map/ppermute | solution.py:50
  94.7 1.0 fusion.14
  95.7 1.4 copy.442
  97.1 0.2 copy.431
  97.4 0.8 copy.417
  98.2 1.5 collective-permute-done.4
  99.7 1.1 broadcast_select_fusion.9
  101.0 0.8 fusion.83
  102.2 1.2 fusion.36
  103.7 10.1 %all_to_all.32 = bf16[16,4,256]{2,0,1:T(8,128)(2,1)S(1)} all-to-all(bf16[16,4,256]{2,0,1:T(8,128)(2,1)S(1)} %copy.436), channel_id=1, replica_groups=mesh['req'=4,'seq'=32] {'req'}, dimensions={1} | all-to-all | bytes 65536 | tf_op jit(solution)/shard_map/all_to_all | solution.py:127
  113.7 1.9 %fusion.149 = f32[64,1024]{1,0:T(8,128)} fusion(bf16[64,256]{1,0:T(8,128)(2,1)S(1)} %bitcast.74, bf16[256,1024]{1,0:T(8,128)(2,1)} %param.29), kind=kOutput, calls=%fused_computation.225 | convolution fusion | flops 33554432 | bytes 819200 | tf_op jit(solution)/shard_map/dot_general | solution.py:129
  115.8 20.7 %reduce-scatter.3.cloned.1.call-done = f32[16,1024]{1,0:T(8,128)} async-done(((f32[64,1024]{1,0:T(8,128)}), f32[16,1024]{1,0:T(8,128)}) %reduce-scatter.3.cloned.1.call-update) | async-done | bytes 65552 | tf_op jit(solution)/shard_map/reduce_scatter | solution.py:128
  136.5 1.0 fusion.139
  137.5 0.2 multiply_reduce_fusion
  137.8 12.0 %all_gather.7 = bf16[64,1024]{1,0:T(8,128)(2,1)S(1)} all-gather(bf16[16,1024]{1,0:T(8,128)(2,1)S(1)} %multiply_convert_fusion), channel_id=1, replica_groups=mesh['req'=4,'seq'=32] {'req'}, dimensions={0}, use_global_device_ids=true | all-gather | bytes 163840 | tf_op jit(solution)/shard_map/all_gather | solution.py:137
  149.8 3.7 %fusion.37 = f32[64,1024]{1,0:T(8,128)} fusion(bf16[1024,1024]{1,0:T(8,128)(2,1)S(1)} %copy-done, bf16[64,1024]{1,0:T(8,128)(2,1)S(1)} %all_gather.7, bf16[1024,1024]{1,0:T(8,128)(2,1)} %param.30), kind=kOutput, calls=%fused_computation.72 | convolution fusion | flops 272695296 | bytes 4587520 | tf_op jit(solution)/shard_map/dot_general | solution.py:144
  153.5 0.6 slice.211
  154.2 0.6 slice.209
  154.8 0.6 slice.207
  155.5 0.6 slice.205
  156.1 18.3 %reduce-scatter.5.cloned.1.call-done = f32[16,1024]{1,0:T(8,128)} async-done(((f32[64,1024]{1,0:T(8,128)}), f32[16,1024]{1,0:T(8,128)}) %reduce-scatter.5.cloned.1.call-update) | async-done | bytes 65552 | tf_op jit(solution)/shard_map/reduce_scatter | solution.py:143
  174.4 0.8 add_convert_fusion
  175.2 0.6 slice.203
  175.9 0.6 slice.201
  (93 shorter events, 3.3 us)
Async XLA Ops:
  7.2 142.6 %copy-start = (bf16[1024,1024]{1,0:T(8,128)(2,1)S(1)}, bf16[1024,1024]{1,0:T(8,128)(2,1)}, u32[]{:S(2)}) copy-start(bf16[1024,1024]{1,0:T(8,128)(2,1)} %param.31) | copy-start | bytes 6291460
  7.2 23.6 %copy-start.14 = (s32[2]{0:T(128)S(1)}, s32[2]{0:T(128)}, u32[]{:S(2)}) copy-start(s32[2]{0:T(128)} %param.22) | copy-start | bytes 28
  7.2 24.3 %copy-start.2 = (bf16[2,256,1024]{2,1,0:T(8,128)(2,1)S(1)}, bf16[2,256,1024]{2,1,0:T(8,128)(2,1)}, u32[]{:S(2)}) copy-start(bf16[2,256,1024]{2,1,0:T(8,128)(2,1)} %param.20) | copy-start | bytes 3145732
  26.5 21.4 %all-to-all-start = ((bf16[4,16,768]{2,1,0:T(8,128)(2,1)}), bf16[4,16,768]{2,1,0:T(8,128)(2,1)S(1)}, u32[]{:S(2)}, u32[]{:S(2)}) async-start(bf16[4,16,768]{2,1,0:T(8,128)(2,1)} %bitcast.75), calls=%async_computation | async-start | bytes 196608 | tf_op jit(solution)/shard_map/all_to_all | solution.py:109
  30.8 105.7 %reduce-scatter.3.cloned.1.call-start = ((), (), s32[]{:S(2)}) async-start(), calls=%async_computation.4 | async-start | bytes 327680 | tf_op jit(solution)/shard_map/reduce_scatter | solution.py:128
  40.6 6.3 %copy-start.15 = (s32[2]{0:T(128)S(1)}, s32[2]{0:T(128)}, u32[]{:S(2)}) copy-start(s32[2]{0:T(128)} %param.23) | copy-start | bytes 28
  51.3 5.6 %copy-start.3 = (bf16[2,4,16,64]{3,2,1,0:T(8,128)(2,1)S(1)}, bf16[2,4,16,64]{3,2,1,0:T(8,128)(2,1)}, u32[]{:S(2)}) copy-start(bf16[2,4,16,64]{3,2,1,0:T(8,128)(2,1)} %slice.164) | copy-start | bytes 49156
  55.4 4.6 %copy-start.8 = (pred[2,1024]{1,0:T(4,128)(4,1)S(1)}, pred[2,1024]{1,0:T(4,128)(4,1)}, u32[]{:S(2)}) copy-start(pred[2,1024]{1,0:T(4,128)(4,1)} %iota_compare_fusion) | copy-start | bytes 6148
  56.7 3.5 %copy-start.1 = (bf16[2,1024,1024]{1,2,0:T(8,128)(2,1)S(1)}, bf16[2,1024,1024]{1,2,0:T(8,128)(2,1)}, u32[]{:S(2)}) copy-start(bf16[2,1024,1024]{1,2,0:T(8,128)(2,1)} %copy.409) | copy-start | bytes 12582916
  56.8 6.6 %collective-permute-start = (f32[2,16,4,66]{1,2,3,0:T(4,128)S(1)}, f32[2,16,4,66]{1,2,3,0:T(4,128)}, u32[]{:S(2)}, u32[]{:S(2)}) collective-permute-start(f32[2,16,4,66]{1,2,3,0:T(4,128)S(1)} %pad_maximum_fusion), channel_id=1, source_target_pairs={{0,1},{1,0},{2,3},{3,2},{4,5},{5,4},{6,7},{7,6},{8,9},{9,8},{10,11... | collective-permute-start | bytes 101384 | tf_op jit(solution)/shard_map/ppermute | solution.py:50
  60.0 1.4 copy-start.9
  60.0 1.4 copy-start.10
  60.2 6.2 %copy-start.13 = (pred[4,4]{1,0:T(4,128)(4,1)S(1)}, pred[4,4]{1,0:T(4,128)(4,1)}, u32[]{:S(2)}) copy-start(pred[4,4]{1,0:T(4,128)(4,1)} %iota_compare_fusion.1) | copy-start | bytes 52
  64.7 8.6 %collective-permute-start.1 = (f32[2,16,4,66]{1,2,3,0:T(4,128)S(1)}, f32[2,16,4,66]{1,2,3,0:T(4,128)S(1)}, u32[]{:S(2)}, u32[]{:S(2)}) collective-permute-start(f32[2,16,4,66]{1,2,3,0:T(4,128)S(1)} %pad_maximum_fusion.1), channel_id=1, source_target_pairs={{0,2},{1,3},{2,0},{3,1},{4,6},{5,7},{6,4},{7,5},{8,10},{9,11},{10,... | collective-permute-start | bytes 101384 | tf_op jit(solution)/shard_map/ppermute | solution.py:50
  73.7 9.4 %collective-permute-start.2 = (f32[2,16,4,66]{1,2,3,0:T(4,128)S(1)}, f32[2,16,4,66]{1,2,3,0:T(4,128)}, u32[]{:S(2)}, u32[]{:S(2)}) collective-permute-start(f32[2,16,4,66]{1,2,3,0:T(4,128)S(1)} %pad_maximum_fusion.2), channel_id=1, source_target_pairs={{0,4},{1,5},{2,6},{3,7},{4,0},{5,1},{6,2},{7,3},{8,12},{9,13},{10,... | collective-permute-start | bytes 101384 | tf_op jit(solution)/shard_map/ppermute | solution.py:50
  84.3 6.9 %collective-permute-start.3 = (f32[2,16,4,66]{1,2,3,0:T(4,128)S(1)}, f32[2,16,4,66]{1,2,3,0:T(4,128)S(1)}, u32[]{:S(2)}, u32[]{:S(2)}) collective-permute-start(f32[2,16,4,66]{1,2,3,0:T(4,128)S(1)} %pad_maximum_fusion.3), channel_id=1, source_target_pairs={{0,8},{1,9},{2,10},{3,11},{4,12},{5,13},{6,14},{7,15},{8,0},{9,1},... | collective-permute-start | bytes 101384 | tf_op jit(solution)/shard_map/ppermute | solution.py:50
  91.4 3.3 %copy-start.11 = (f32[2,16,4,1]{1,2,3,0:T(4,128)}, f32[2,16,4,1]{1,2,3,0:T(4,128)S(1)}, u32[]{:S(2)}) copy-start(f32[2,16,4,1]{1,2,3,0:T(4,128)S(1)} %get-tuple-element.34) | copy-start | bytes 1540
  91.6 8.1 %collective-permute-start.4 = (f32[2,16,4,66]{1,2,3,0:T(4,128)S(1)}, f32[2,16,4,66]{1,2,3,0:T(4,128)}, u32[]{:S(2)}, u32[]{:S(2)}) collective-permute-start(f32[2,16,4,66]{1,2,3,0:T(4,128)S(1)} %pad_maximum_fusion.4), channel_id=1, source_target_pairs={{0,16},{1,17},{2,18},{3,19},{4,20},{5,21},{6,22},{7,23},{8,24},{9,... | collective-permute-start | bytes 101384 | tf_op jit(solution)/shard_map/ppermute | solution.py:50
  97.1 40.5 %copy-start.12 = (f32[1024]{0:T(1024)S(1)}, f32[1024]{0:T(1024)}, u32[]{:S(2)}) copy-start(f32[1024]{0:T(1024)} %param.25) | copy-start | bytes 12292
  115.7 58.7 %reduce-scatter.5.cloned.1.call-start = ((), (), s32[]{:S(2)}) async-start(), calls=%async_computation.5 | async-start | bytes 327680 | tf_op jit(solution)/shard_map/reduce_scatter | solution.py:143
  149.8 3.8 %copy-start.7 = (bf16[8,4,1,256]{3,2,0,1:T(2,128)(2,1)S(1)}, bf16[8,4,1,256]{3,2,0,1:T(2,128)(2,1)}, u32[]{:S(2)}) copy-start(bf16[8,4,1,256]{3,2,0,1:T(2,128)(2,1)} %get-tuple-element.41) | copy-start | bytes 49156
  149.8 4.4 %copy-start.6 = (bf16[8,4,1,256]{3,2,0,1:T(2,128)(2,1)S(1)}, bf16[8,4,1,256]{3,2,0,1:T(2,128)(2,1)}, u32[]{:S(2)}) copy-start(bf16[8,4,1,256]{3,2,0,1:T(2,128)(2,1)} %get-tuple-element.42) | copy-start | bytes 49156
  149.8 5.0 %copy-start.5 = (bf16[8,4,1,256]{3,2,0,1:T(2,128)(2,1)S(1)}, bf16[8,4,1,256]{3,2,0,1:T(2,128)(2,1)}, u32[]{:S(2)}) copy-start(bf16[8,4,1,256]{3,2,0,1:T(2,128)(2,1)} %get-tuple-element.43) | copy-start | bytes 49156
  149.8 5.7 %copy-start.4 = (bf16[8,4,1,256]{3,2,0,1:T(2,128)(2,1)S(1)}, bf16[8,4,1,256]{3,2,0,1:T(2,128)(2,1)}, u32[]{:S(2)}) copy-start(bf16[8,4,1,256]{3,2,0,1:T(2,128)(2,1)} %get-tuple-element.44) | copy-start | bytes 49156
Sparse Core Ops, SparseCore 0:
  115.8 20.6 reduce-scatter.2
  153.6 20.6 reduce-scatter.4

commit v3 on v2

--- a/solution.py
+++ b/solution.py
@@ -18,15 +18,31 @@
 
 
 def partial_block(query, keys, values, valid):
-    scores = jnp.einsum("rthd,rphd->rhtp", query, keys, preferred_element_type=jnp.float32) * 0.125
+    scores = jnp.einsum("rthd,rphd->rthp", query, keys, preferred_element_type=jnp.float32) * 0.125
     scores = jnp.where(valid, scores, masked_score)
     peak = jnp.max(scores, axis=-1)
     weights = jnp.where(valid, jnp.exp(scores - peak[..., None]), 0.0)
     total = jnp.sum(weights, axis=-1)
     output = jnp.einsum(
-        "rhtp,rphd->rhtd", weights.astype(jnp.bfloat16), values, preferred_element_type=jnp.float32
+        "rthp,rphd->rthd", weights.astype(jnp.bfloat16), values, preferred_element_type=jnp.float32
     )
     return (peak, total, output)
+
+
+def cache_block(query, keys, values, valid):
+    reqs, steps = query.shape[0], query.shape[1]
+    eye = jnp.eye(H, dtype=query.dtype)
+    spread = (query[:, :, :, None, :] * eye[None, None, :, :, None]).reshape(reqs, steps * H, H * HD)
+    scores = jnp.einsum("rnc,rpc->rnp", spread, keys, preferred_element_type=jnp.float32) * 0.125
+    scores = jnp.where(valid, scores, masked_score)
+    peak = jnp.max(scores, axis=-1)
+    weights = jnp.where(valid, jnp.exp(scores - peak[..., None]), 0.0)
+    total = jnp.sum(weights, axis=-1)
+    full = jnp.einsum(
+        "rnp,rpc->rnc", weights.astype(jnp.bfloat16), values, preferred_element_type=jnp.float32
+    ).reshape(reqs, steps, H, H, HD)
+    output = jnp.sum(full * eye.astype(jnp.float32)[None, None, :, :, None], axis=3)
+    return (peak.reshape(reqs, steps, H), total.reshape(reqs, steps, H), output)
 
 
 def join(first, second):
@@ -88,16 +104,13 @@
     groups = lax.axis_size("req")
     block = long_keys.shape[1]
     anchor = lax.axis_index("seq") * block
-    cache_short_k = short_keys.reshape(short_count, short_keys.shape[1], H, HD)
-    cache_short_v = short_values.reshape(short_count, short_keys.shape[1], H, HD)
-    cache_long_k = long_keys.reshape(long_count, block, H, HD)
-    cache_long_v = long_values.reshape(long_count, block, H, HD)
-    short_valid = (jnp.arange(short_keys.shape[1])[None, :] < short_lengths[:, None])[:, None, None, :]
-    long_valid = ((anchor + jnp.arange(block))[None, :] < long_lengths[:, None])[:, None, None, :]
+    short_valid = (jnp.arange(short_keys.shape[1])[None, :] < short_lengths[:, None])[:, None, :]
+    long_valid = ((anchor + jnp.arange(block))[None, :] < long_lengths[:, None])[:, None, :]
+    w_out_full = lax.all_gather(w_out, "req", axis=0, tiled=True)
     stacked = jnp.concatenate([w_query, w_key, w_value], 1)
     local = w_query.shape[1]
     fresh_ids = jnp.arange(steps)
-    fresh_valid = (fresh_ids[None, :] <= fresh_ids[:, None])[None, None, :, :]
+    fresh_valid = (fresh_ids[None, :] <= fresh_ids[:, None])[None, :, None, :]
 
     rows = jnp.concatenate([short_tokens, long_tokens], 0).reshape(rows_count, width).astype(jnp.float32)
     normed = layer_norm(rows, attn_gain).astype(jnp.bfloat16)
@@ -114,23 +127,17 @@
     fresh_k = key_now.reshape(req_count, steps, H, HD)
     fresh_v = value_now.reshape(req_count, steps, H, HD)
     fresh = partial_block(query, fresh_k, fresh_v, fresh_valid)
-    short_part = partial_block(query[:short_count], cache_short_k, cache_short_v, short_valid)
+    short_part = cache_block(query[:short_count], short_keys, short_values, short_valid)
     long_part = merge_long(
-        partial_block(query[short_count:], cache_long_k, cache_long_v, long_valid)
+        cache_block(query[short_count:], long_keys, long_values, long_valid)
     )
     cache_part = jax.tree.map(
         lambda first, second: jnp.concatenate([first, second], 0), short_part, long_part
     )
     peak, total, output = join(cache_part, fresh)
     attended = output / total[..., None]
-    attended = attended.transpose(0, 2, 1, 3).reshape(rows_count, width).astype(jnp.bfloat16)
-    spread = lax.all_to_all(attended, "req", split_axis=1, concat_axis=0, tiled=True)
-    mixed = rows + lax.psum_scatter(
-        jnp.dot(spread, w_out, preferred_element_type=jnp.float32),
-        "req",
-        scatter_dimension=0,
-        tiled=True,
-    )
+    attended = attended.reshape(rows_count, width).astype(jnp.bfloat16)
+    mixed = rows + jnp.dot(attended, w_out_full, preferred_element_type=jnp.float32)
     normed_ffn = layer_norm(mixed, ffn_gain).astype(jnp.bfloat16)
     hidden = jax.nn.gelu(
         jnp.dot(

time: 185 us -> 144 us (0.78)
  local copies, waits for them, and re-layouts: 30 us -> 12.2 us
  waiting for transfers between devices: 56.2 us -> 45.9 us
  blocking collectives: 35.4 us -> 25.3 us
  other arithmetic: 16.3 us -> 13.9 us
    reduce_scatter x1 -> x0, waiting for transfers between devices: 20.7 us -> none  [shards(): lax.psum_scatter(jnp.dot(spread, w_out, preferred_element_type=jnp.float3...]
    unnamed x38 -> x36, local copies, waits for them, and re-layouts: 17.1 us -> 0.09 us
    all_to_all x1 -> x0, blocking collectives: 10.1 us -> none  [shards(): lax.all_to_all(attended, 'req', split_axis=1, concat_axis=0, tiled=True)]
    ppermute x5, waiting for transfers between devices: 17.2 us -> 22.6 us  [merge_long(): other = lax.ppermute(packed, 'seq', pairs)]
    all_to_all x1, waiting for transfers between devices: 0.01 us -> 4 us  [shards(): lax.all_to_all(project_spread, 'req', split_axis=0, concat_axis=1, tiled=...]
    reduce_sum x0 -> x3, other arithmetic: none -> 2.54 us  [the longest x1 2.13 us: cache_block(): jnp.sum(full * eye.astype(jnp.float32)[None, None, :, :, None], axis=3)]
    reshape x0 -> x2, local copies, waits for them, and re-layouts: none -> 2.53 us  [cache_block(): full = jnp.einsum('rnp,rpc->rnc', weights.astype(jnp.bfloat16), values, p...]
    dot_general x4 -> x2, local copies, waits for them, and re-layouts: 2.3 us -> 0.41 us  [the longest x1 0.24 us: partial_block(): jnp.einsum('rthp,rphd->rthd', weights.astype(jnp.bfloat16), values, prefe...]
  transfers between devices with their start and end apart: 8 -> 8, of which waited for: 6 -> 6; matrix products, arithmetic and copies ran while one was open for 18% -> 21% of each run, Pallas kernels for 0% -> 0%
where the time goes in v3:
time: 144 us
  waiting for transfers between devices  45.9 us (32%)
  blocking collectives  25.3 us (18%)
  matrix products  17.7 us (12%)
  between operations  14.6 us (10%)
  other arithmetic  13.9 us (10%)
  starting transfers between devices  13.9 us (10%)
  local copies, waits for them, and re-layouts  12.2 us (8%)
    ppermute x5, waiting for transfers between devices, merge_long(): other = lax.ppermute(packed, 'seq', pairs)  22.6 us
    reduce_scatter x1, waiting for transfers between devices, shards(): lax.psum_scatter(jnp.dot(hidden, w_down, preferred_element_type=jnp.float...  18.5 us
    all_gather x1, blocking collectives, shards(): lax.all_gather(normed, 'req', axis=0, tiled=True)  13.3 us
    all_gather x1, blocking collectives, shards(): lax.all_gather(normed_ffn, 'req', axis=0, tiled=True)  12 us
    ppermute x5, starting transfers between devices, merge_long(): other = lax.ppermute(packed, 'seq', pairs)  9.6 us
    dot_general x2, matrix products, cache_block(): jnp.einsum('rnc,rpc->rnp', spread, keys, preferred_element_type=jnp.float32)  5.82 us
    all_to_all x1, starting transfers between devices, shards(): lax.all_to_all(project_spread, 'req', split_axis=0, concat_axis=1, tiled=...  4.26 us
    all_to_all x1, waiting for transfers between devices, shards(): lax.all_to_all(project_spread, 'req', split_axis=0, concat_axis=1, tiled=...  4 us
  transfers between devices with their start and end apart: 8, of which 6 were waited for; matrix products, arithmetic and copies ran while one was open for 21% of the time, Pallas kernels for 0%

profile of v3, /device:TPU:0, one launch (start us, length us, event | category | flops | bytes accessed | tf_op | source)
XLA Modules:
  0.0 143.6 jit_solution(11437856707310155101)
XLA Ops:
  7.2 0.9 maximum_convert_fusion
  8.1 0.8 fusion.141
  8.9 0.9 multiply_reduce_fusion.3
  10.1 0.8 multiply_convert_fusion.1
  10.8 13.3 %all_gather.9 = bf16[64,1024]{1,0:T(8,128)(2,1)S(1)} all-gather(bf16[16,1024]{1,0:T(8,128)(2,1)S(1)} %multiply_convert_fusion.1), channel_id=1, replica_groups=mesh['req'=4,'seq'=32] {'req'}, dimensions={0}, use_global_device_ids=true | all-gather | bytes 163840 | tf_op jit(solution)/shard_map/all_gather | solution.py:118
  24.1 2.4 %fusion.7 = bf16[64,768]{1,0:T(8,128)(2,1)} fusion(bf16[64,1024]{1,0:T(8,128)(2,1)S(1)} %all_gather.9, bf16[1024,256]{1,0:T(8,128)(2,1)} %param.28, bf16[1024,256]{1,0:T(8,128)(2,1)} %param.27, bf16[1024,256]{1,0:T(8,128)(2,1)} %param.26), kind=kOutput, calls=%fused_computation.8 | convolution fusion | flops 105431040 | bytes 1802240 | tf_op jit(solution)/shard_map/dot_general | solution.py:117
  26.5 4.3 %all-to-all-start = ((bf16[4,16,768]{2,1,0:T(8,128)(2,1)}), bf16[4,16,768]{2,1,0:T(8,128)(2,1)S(1)}, u32[]{:S(2)}, u32[]{:S(2)}) async-start(bf16[4,16,768]{2,1,0:T(8,128)(2,1)} %bitcast), calls=%async_computation | async-start | bytes 196608 | tf_op jit(solution)/shard_map/all_to_all | solution.py:122
  30.8 0.7 all-gather.2.cloned.1.call-update
  31.7 0.2 mul.307
  32.1 0.5 iota_compare_fusion.2
  32.6 4.0 %all-to-all-done = bf16[4,16,768]{2,1,0:T(8,128)(2,1)S(1)} async-done(((bf16[4,16,768]{2,1,0:T(8,128)(2,1)}), bf16[4,16,768]{2,1,0:T(8,128)(2,1)S(1)}, u32[]{:S(2)}, u32[]{:S(2)}) %all-to-all-start) | async-done | bytes 98336 | tf_op jit(solution)/shard_map/all_to_all | solution.py:122
  36.6 0.8 fusion.144
  37.5 0.8 fusion.145
  38.5 0.3 mul.317
  38.8 1.8 %fusion.147 = (f32[2,64]{1,0:T(2,128)S(1)}, f32[2,64,256]{2,1,0:T(8,128)S(1)}) fusion(bf16[2,256,1024]{2,1,0:T(8,128)(2,1)} %param.20, bf16[2,64,1024]{2,1,0:T(8,128)(2,1)S(1)} %mul.317, bf16[64,1024]{1,0:T(8,128)(2,1)S(1)} %mul.307, pred[2,256]{1,0:T(4,128)(4,1)S(1)} %broadcast_compare_fusion), kind=kOutput, calls=%fused_computation.229 | convolution fusion | flops 67338112 | bytes 1573888 | tf_op jit(solution)/shard_map/rnc,rpc->rnp/dot_general | solution.py:36
  40.7 0.2 fusion.72
  40.8 1.6 %fusion.74 = f32[2,64,1024]{2,1,0:T(8,128)S(1)} fusion(bf16[2,256,1024]{2,1,0:T(8,128)(2,1)} %param.21, f32[2,64,256]{2,1,0:T(8,128)S(1)} %get-tuple-element.55, f32[2,64]{1,0:T(2,128)S(1)} %get-tuple-element.54, pred[2,256]{1,0:T(4,128)(4,1)S(1)} %broadcast_compare_fusion), kind=kOutput, calls=%fused_computation.113 | convolution fusion | flops 67207168 | bytes 1704960 | tf_op jit(solution)/shard_map/rnp,rpc->rnc/dot_general | solution.py:41
  42.4 1.3 reshape.257
  43.9 0.3 mul.305
  44.3 4.1 %fusion.148 = (f32[2,64]{1,0:T(2,128)S(1)}, f32[2,64,1024]{2,1,0:T(8,128)S(1)}) fusion(bf16[2,1024,1024]{2,1,0:T(8,128)(2,1)} %param.18, bf16[2,64,1024]{2,1,0:T(8,128)(2,1)S(1)} %mul.305, bf16[64,1024]{1,0:T(8,128)(2,1)S(1)} %mul.307, pred[2,1024]{1,0:T(4,128)(4,1)S(1)} %iota_compare_fusion.1), kind=kOutput, calls=%fused_computation.230 | convolution fusion | flops 268959616 | bytes 5114368 | tf_op jit(solution)/shard_map/rnc,rpc->rnp/dot_general | solution.py:36
  48.3 0.9 fusion.19
  49.3 1.2 reshape.256
  50.5 2.1 %multiply_reduce_fusion.1 = (f32[2,4,16,64]{3,2,1,0:T(8,128)S(1)}, f32[2,4,16,64]{3,2,1,0:T(8,128)S(1)}) fusion(f32[2,4,16,16,64]{4,3,2,1,0:T(8,128)} %reshape.256, f32[16,16]{1,0:T(8,128)S(1)} %fusion.97, f32[2,4,16,16,64]{4,3,2,1,0:T(8,128)} %reshape.257), kind=kLoop, calls=%fused_computation.13 | loop fusion | flops 507904 | bytes 1115136 | tf_op jit(solution)/shard_map/reduce_sum | solution.py:44
  52.7 0.1 copy.305
  53.1 0.1 reshape_reshape_squeeze.6
  53.3 0.7 reshape_squeeze.2
  54.0 1.0 fusion.78
  55.1 0.2 copy.313
  55.2 1.1 broadcast_select_fusion.1
  56.5 1.7 %collective-permute-start.1 = (f32[2,4,16,66]{2,1,3,0:T(4,128)S(1)}, f32[2,4,16,66]{2,1,3,0:T(4,128)S(1)}, u32[]{:S(2)}, u32[]{:S(2)}) collective-permute-start(f32[2,4,16,66]{2,1,3,0:T(4,128)S(1)} %pad_maximum_fusion.1), channel_id=1, source_target_pairs={{0,2},{1,3},{2,0},{3,1},{4,6},{5,7},{6,4},{7,5},{8,10},{9,11},{10,... | collective-permute-start | bytes 101384 | tf_op jit(solution)/shard_map/ppermute | solution.py:66
  58.2 0.1 fusion.84
  58.3 7.2 %collective-permute-done.1 = f32[2,4,16,66]{2,1,3,0:T(4,128)S(1)} collective-permute-done((f32[2,4,16,66]{2,1,3,0:T(4,128)S(1)}, f32[2,4,16,66]{2,1,3,0:T(4,128)S(1)}, u32[]{:S(2)}, u32[]{:S(2)}) %collective-permute-start.1) | collective-permute-done | bytes 33824 | tf_op jit(solution)/shard_map/ppermute | solution.py:66
  65.5 0.1 broadcast_select_fusion.3
  65.8 3.3 %collective-permute-start.2 = (f32[2,4,16,66]{2,1,3,0:T(4,128)S(1)}, f32[2,4,16,66]{2,1,3,0:T(4,128)}, u32[]{:S(2)}, u32[]{:S(2)}) collective-permute-start(f32[2,4,16,66]{2,1,3,0:T(4,128)S(1)} %pad_maximum_fusion.2), channel_id=1, source_target_pairs={{0,4},{1,5},{2,6},{3,7},{4,0},{5,1},{6,2},{7,3},{8,12},{9,13},{10,... | collective-permute-start | bytes 101384 | tf_op jit(solution)/shard_map/ppermute | solution.py:66
  69.1 0.7 fusion.85
  69.8 0.2 copy.319
  70.2 5.5 %collective-permute-done.2 = f32[2,4,16,66]{2,1,3,0:T(4,128)} collective-permute-done((f32[2,4,16,66]{2,1,3,0:T(4,128)S(1)}, f32[2,4,16,66]{2,1,3,0:T(4,128)}, u32[]{:S(2)}, u32[]{:S(2)}) %collective-permute-start.2) | collective-permute-done | bytes 33824 | tf_op jit(solution)/shard_map/ppermute | solution.py:66
  75.6 1.1 broadcast_select_fusion.5
  76.9 1.6 %collective-permute-start.3 = (f32[2,4,16,66]{2,1,3,0:T(4,128)S(1)}, f32[2,4,16,66]{2,1,3,0:T(4,128)S(1)}, u32[]{:S(2)}, u32[]{:S(2)}) collective-permute-start(f32[2,4,16,66]{2,1,3,0:T(4,128)S(1)} %pad_maximum_fusion.3), channel_id=1, source_target_pairs={{0,8},{1,9},{2,10},{3,11},{4,12},{5,13},{6,14},{7,15},{8,0},{9,1},... | collective-permute-start | bytes 101384 | tf_op jit(solution)/shard_map/ppermute | solution.py:66
  78.5 0.2 fusion.76
  78.7 5.6 %collective-permute-done.3 = f32[2,4,16,66]{2,1,3,0:T(4,128)S(1)} collective-permute-done((f32[2,4,16,66]{2,1,3,0:T(4,128)S(1)}, f32[2,4,16,66]{2,1,3,0:T(4,128)S(1)}, u32[]{:S(2)}, u32[]{:S(2)}) %collective-permute-start.3) | collective-permute-done | bytes 33824 | tf_op jit(solution)/shard_map/ppermute | solution.py:66
  84.2 0.1 broadcast_select_fusion.7
  84.5 0.8 pad_maximum_fusion.4
  85.3 3.0 %collective-permute-start.4 = (f32[2,4,16,66]{2,1,3,0:T(4,128)}, f32[2,4,16,66]{2,1,3,0:T(4,128)}, u32[]{:S(2)}, u32[]{:S(2)}) collective-permute-start(f32[2,4,16,66]{2,1,3,0:T(4,128)} %pad_maximum_fusion.4), channel_id=1, source_target_pairs={{0,16},{1,17},{2,18},{3,19},{4,20},{5,21},{6,22},{7,23},{8,24},{9,... | collective-permute-start | bytes 101384 | tf_op jit(solution)/shard_map/ppermute | solution.py:66
  88.3 0.2 fusion.14
  88.7 0.2 copy.308
  88.9 0.2 copy.320
  89.1 4.5 %collective-permute-done.4 = f32[2,4,16,66]{2,1,3,0:T(4,128)} collective-permute-done((f32[2,4,16,66]{2,1,3,0:T(4,128)}, f32[2,4,16,66]{2,1,3,0:T(4,128)}, u32[]{:S(2)}, u32[]{:S(2)}) %collective-permute-start.4) | collective-permute-done | bytes 33824 | tf_op jit(solution)/shard_map/ppermute | solution.py:66
  93.6 1.1 broadcast_select_fusion.9
  94.8 0.2 fusion.13
  95.1 0.1 copy.324
  95.2 0.1 convert_element_type.78
  95.4 2.1 %fusion.149 = (f32[16]{0:T(128)S(1)}, f32[16,1024]{1,0:T(8,128)S(1)}) fusion(f32[16,1024]{1,0:T(8,128)S(1)} %reshape.258, bf16[16,1024]{1,0:T(8,128)(2,1)S(1)} %convert_element_type.78, bf16[1024,1024]{1,0:T(8,128)(2,1)} %all-gather.2.cloned.1.call-done), kind=kOutput, calls=%fused_computation.231 | convolution fusion | flops 33587184 | bytes 2261056 | tf_op jit(solution)/shard_map/dot_general | solution.py:140
  97.5 0.2 multiply_reduce_fusion.2
  97.8 12.0 %all_gather.11 = bf16[64,1024]{1,0:T(8,128)(2,1)S(1)} all-gather(bf16[16,1024]{1,0:T(8,128)(2,1)S(1)} %multiply_convert_fusion), channel_id=1, replica_groups=mesh['req'=4,'seq'=32] {'req'}, dimensions={0}, use_global_device_ids=true | all-gather | bytes 163840 | tf_op jit(solution)/shard_map/all_gather | solution.py:144
  109.8 3.7 %fusion.38 = f32[64,1024]{1,0:T(8,128)} fusion(bf16[1024,1024]{1,0:T(8,128)(2,1)S(1)} %copy-done, bf16[64,1024]{1,0:T(8,128)(2,1)S(1)} %all_gather.11, bf16[1024,1024]{1,0:T(8,128)(2,1)} %param.30), kind=kOutput, calls=%fused_computation.77 | convolution fusion | flops 272695296 | bytes 4587520 | tf_op jit(solution)/shard_map/dot_general | solution.py:151
  113.6 0.6 slice.199
  114.2 0.6 slice.201
  114.8 0.6 slice.203
  115.5 0.6 slice.205
  116.1 18.5 %reduce-scatter.2.cloned.1.call-done = f32[16,1024]{1,0:T(8,128)} async-done(((f32[64,1024]{1,0:T(8,128)}), f32[16,1024]{1,0:T(8,128)}) %reduce-scatter.2.cloned.1.call-update) | async-done | bytes 65552 | tf_op jit(solution)/shard_map/reduce_scatter | solution.py:150
  134.6 0.8 add_convert_fusion
  135.5 0.6 slice.195
  136.1 0.6 slice.197
  (96 shorter events, 2.7 us)
Async XLA Ops:
  7.2 102.6 %copy-start = (bf16[1024,1024]{1,0:T(8,128)(2,1)S(1)}, bf16[1024,1024]{1,0:T(8,128)(2,1)}, u32[]{:S(2)}) copy-start(bf16[1024,1024]{1,0:T(8,128)(2,1)} %param.31) | copy-start | bytes 6291460
  24.1 7.8 %copy-start.16 = (s32[2]{0:T(128)S(1)}, s32[2]{0:T(128)}, u32[]{:S(2)}) copy-start(s32[2]{0:T(128)} %param.22) | copy-start | bytes 28
  24.1 7.9 %copy-start.17 = (s32[2]{0:T(128)S(1)}, s32[2]{0:T(128)}, u32[]{:S(2)}) copy-start(s32[2]{0:T(128)} %param.23) | copy-start | bytes 28
  26.5 10.1 %all-to-all-start = ((bf16[4,16,768]{2,1,0:T(8,128)(2,1)}), bf16[4,16,768]{2,1,0:T(8,128)(2,1)S(1)}, u32[]{:S(2)}, u32[]{:S(2)}) async-start(bf16[4,16,768]{2,1,0:T(8,128)(2,1)} %bitcast), calls=%async_computation | async-start | bytes 196608 | tf_op jit(solution)/shard_map/all_to_all | solution.py:122
  30.8 64.6 %all-gather.2.cloned.1.call-start = ((), (), s32[]{:S(2)}) async-start(), calls=%async_computation.2 | async-start | bytes 2621440 | tf_op jit(solution)/shard_map/all_gather | solution.py:109
  31.5 103.1 %reduce-scatter.2.cloned.1.call-start = ((), (), s32[]{:S(2)}) async-start(), calls=%async_computation.3 | async-start | bytes 327680 | tf_op jit(solution)/shard_map/reduce_scatter | solution.py:150
  44.2 4.1 %copy-start.1 = (bf16[2,1024,1024]{2,1,0:T(8,128)(2,1)S(1)}, bf16[2,1024,1024]{2,1,0:T(8,128)(2,1)}, u32[]{:S(2)}) copy-start(bf16[2,1024,1024]{2,1,0:T(8,128)(2,1)} %param.19) | copy-start | bytes 12582916
  48.3 0.9 copy-start.12
  50.5 2.6 %copy-start.4 = (bf16[16,4,1,256]{3,2,0,1:T(2,128)(2,1)S(1)}, bf16[16,4,1,256]{3,2,0,1:T(2,128)(2,1)}, u32[]{:S(2)}) copy-start(bf16[16,4,1,256]{3,2,0,1:T(2,128)(2,1)} %get-tuple-element.47) | copy-start | bytes 98308
  50.5 2.7 %copy-start.3 = (bf16[16,4,1,256]{3,2,0,1:T(2,128)(2,1)S(1)}, bf16[16,4,1,256]{3,2,0,1:T(2,128)(2,1)}, u32[]{:S(2)}) copy-start(bf16[16,4,1,256]{3,2,0,1:T(2,128)(2,1)} %get-tuple-element.46) | copy-start | bytes 98308
  52.6 5.6 %copy-start.15 = (pred[4,4]{1,0:T(4,128)(4,1)S(1)}, pred[4,4]{1,0:T(4,128)(4,1)}, u32[]{:S(2)}) copy-start(pred[4,4]{1,0:T(4,128)(4,1)} %iota_compare_fusion.2) | copy-start | bytes 52
  53.0 2.2 %collective-permute-start = (f32[2,4,16,66]{2,1,3,0:T(4,128)S(1)}, f32[2,4,16,66]{2,1,3,0:T(4,128)}, u32[]{:S(2)}, u32[]{:S(2)}) collective-permute-start(f32[2,4,16,66]{2,1,3,0:T(4,128)S(1)} %pad_maximum_fusion), channel_id=1, source_target_pairs={{0,1},{1,0},{2,3},{3,2},{4,5},{5,4},{6,7},{7,6},{8,9},{9,8},{10,11... | collective-permute-start | bytes 101384 | tf_op jit(solution)/shard_map/ppermute | solution.py:66
  56.3 13.7 %copy-start.2 = (bf16[16,4,1,256]{3,2,0,1:T(2,128)(2,1)S(1)}, bf16[16,4,1,256]{3,2,0,1:T(2,128)(2,1)}, u32[]{:S(2)}) copy-start(bf16[16,4,1,256]{3,2,0,1:T(2,128)(2,1)} %get-tuple-element.45) | copy-start | bytes 98308
  56.5 8.9 %collective-permute-start.1 = (f32[2,4,16,66]{2,1,3,0:T(4,128)S(1)}, f32[2,4,16,66]{2,1,3,0:T(4,128)S(1)}, u32[]{:S(2)}, u32[]{:S(2)}) collective-permute-start(f32[2,4,16,66]{2,1,3,0:T(4,128)S(1)} %pad_maximum_fusion.1), channel_id=1, source_target_pairs={{0,2},{1,3},{2,0},{3,1},{4,6},{5,7},{6,4},{7,5},{8,10},{9,11},{10,... | collective-permute-start | bytes 101384 | tf_op jit(solution)/shard_map/ppermute | solution.py:66
  58.3 11.5 %copy-start.9 = (f32[4,4,16]{2,1,0:T(4,128)}, f32[4,4,16]{2,1,0:T(4,128)S(1)}, u32[]{:S(2)}) copy-start(f32[4,4,16]{2,1,0:T(4,128)S(1)} %fusion.84) | copy-start | bytes 3076
  65.8 9.8 %collective-permute-start.2 = (f32[2,4,16,66]{2,1,3,0:T(4,128)S(1)}, f32[2,4,16,66]{2,1,3,0:T(4,128)}, u32[]{:S(2)}, u32[]{:S(2)}) collective-permute-start(f32[2,4,16,66]{2,1,3,0:T(4,128)S(1)} %pad_maximum_fusion.2), channel_id=1, source_target_pairs={{0,4},{1,5},{2,6},{3,7},{4,0},{5,1},{6,2},{7,3},{8,12},{9,13},{10,... | collective-permute-start | bytes 101384 | tf_op jit(solution)/shard_map/ppermute | solution.py:66
  76.7 11.6 %copy-start.13 = (f32[2,64]{1,0:T(2,128)S(1)}, f32[2,64]{1,0:T(2,128)}, u32[]{:S(2)}) copy-start(f32[2,64]{1,0:T(2,128)} %copy-done.12) | copy-start | bytes 1540
  76.9 7.3 %collective-permute-start.3 = (f32[2,4,16,66]{2,1,3,0:T(4,128)S(1)}, f32[2,4,16,66]{2,1,3,0:T(4,128)S(1)}, u32[]{:S(2)}, u32[]{:S(2)}) collective-permute-start(f32[2,4,16,66]{2,1,3,0:T(4,128)S(1)} %pad_maximum_fusion.3), channel_id=1, source_target_pairs={{0,8},{1,9},{2,10},{3,11},{4,12},{5,13},{6,14},{7,15},{8,0},{9,1},... | collective-permute-start | bytes 101384 | tf_op jit(solution)/shard_map/ppermute | solution.py:66
  84.4 10.3 %copy-start.10 = (f32[4,4,16]{2,1,0:T(4,128)S(1)}, f32[4,4,16]{2,1,0:T(4,128)}, u32[]{:S(2)}) copy-start(f32[4,4,16]{2,1,0:T(4,128)} %copy-done.9) | copy-start | bytes 3076
  84.4 10.3 %copy-start.11 = (f32[4,4,16]{2,1,0:T(4,128)S(1)}, f32[4,4,16]{2,1,0:T(4,128)}, u32[]{:S(2)}) copy-start(f32[4,4,16]{2,1,0:T(4,128)} %get-tuple-element.48) | copy-start | bytes 3076
  85.3 8.3 %collective-permute-start.4 = (f32[2,4,16,66]{2,1,3,0:T(4,128)}, f32[2,4,16,66]{2,1,3,0:T(4,128)}, u32[]{:S(2)}, u32[]{:S(2)}) collective-permute-start(f32[2,4,16,66]{2,1,3,0:T(4,128)} %pad_maximum_fusion.4), channel_id=1, source_target_pairs={{0,16},{1,17},{2,18},{3,19},{4,20},{5,21},{6,22},{7,23},{8,24},{9,... | collective-permute-start | bytes 101384 | tf_op jit(solution)/shard_map/ppermute | solution.py:66
  94.8 2.9 %copy-start.14 = (f32[1024]{0:T(1024)S(1)}, f32[1024]{0:T(1024)}, u32[]{:S(2)}) copy-start(f32[1024]{0:T(1024)} %param.25) | copy-start | bytes 12292
  109.8 3.8 %copy-start.8 = (bf16[8,4,1,256]{3,2,0,1:T(2,128)(2,1)S(1)}, bf16[8,4,1,256]{3,2,0,1:T(2,128)(2,1)}, u32[]{:S(2)}) copy-start(bf16[8,4,1,256]{3,2,0,1:T(2,128)(2,1)} %get-tuple-element.42) | copy-start | bytes 49156
  109.8 4.4 %copy-start.7 = (bf16[8,4,1,256]{3,2,0,1:T(2,128)(2,1)S(1)}, bf16[8,4,1,256]{3,2,0,1:T(2,128)(2,1)}, u32[]{:S(2)}) copy-start(bf16[8,4,1,256]{3,2,0,1:T(2,128)(2,1)} %get-tuple-element.41) | copy-start | bytes 49156
  109.8 5.0 %copy-start.6 = (bf16[8,4,1,256]{3,2,0,1:T(2,128)(2,1)S(1)}, bf16[8,4,1,256]{3,2,0,1:T(2,128)(2,1)}, u32[]{:S(2)}) copy-start(bf16[8,4,1,256]{3,2,0,1:T(2,128)(2,1)} %get-tuple-element.40) | copy-start | bytes 49156
  109.8 5.7 %copy-start.5 = (bf16[8,4,1,256]{3,2,0,1:T(2,128)(2,1)S(1)}, bf16[8,4,1,256]{3,2,0,1:T(2,128)(2,1)}, u32[]{:S(2)}) copy-start(bf16[8,4,1,256]{3,2,0,1:T(2,128)(2,1)} %get-tuple-element.39) | copy-start | bytes 49156
Sparse Core Ops, SparseCore 0:
  33.3 32.8 all-gather.1
  113.7 20.9 reduce-scatter.1
